TPU v7x, 512 devices: a whole 4x4x16 slice. The times are simulated.
512 devices in a mesh: dp: 8 (over x, core), tensor: 64 (over z, y).
Axes of the slice: x: 4, y: 4, z: 16, core: 2. Of those that a mesh axis runs over, the one named last changes fastest.
Arguments:
- states: bfloat16 [65536, 2048], P(('dp', 'tensor')), may hold values from -150 to 150
- norm_gain: float32 [2048], replicated, may hold values from 0.1 to 1.9
- norm_bias: float32 [2048], replicated, may hold values from -3 to 3
- head_table: bfloat16 [250880, 2048], P('tensor', 'dp'), may hold values from -2 to 2
- seq_lengths: int32 [8], P('dp'), may hold values from 4096 to 8192
- scored_index: int32 [2048], P('dp'), may hold values from 0 to 8191
- targets: int32 [2048], P('dp'), may hold values from 0 to 250879
- slot_mask: int32 [2048], P('dp'), may hold values 0 or 1
Outputs:
- logprob: float32 [2048], P(('dp', 'tensor'))
- entropy: float32 [2048], P(('dp', 'tensor'))
All inputs are finite; a program needn't handle non-finite values. No bound on the sum of `slot_mask` on one device may be relied on, other than what follows from the above.
Results may differ from a plain program's by a relative error of at most 0.012.
The roundings to bfloat16 on the way count: a program that leaves them out, or rounds other values in their place, can miss the bound.
Values may be sent and summed in bfloat16 or wider, within the bound.
No kernel may reach another device: no remote copies, remote signals or barrier semaphores. Data moves between devices by JAX's collectives and lax.ppermute only.
A program may use at most 64 MiB of HBM per device.

v0:
```python
import jax
import jax.numpy as jnp
from jax import lax
from jax.sharding import PartitionSpec as P

EPSILON = 1e-05


def layer_norm(states, norm_gain, norm_bias):
    values = states.astype(jnp.float32)
    center = jnp.mean(values, axis=1, keepdims=True)
    shifted = values - center
    variance = jnp.mean(shifted * shifted, axis=1, keepdims=True)
    return (shifted * lax.rsqrt(variance + EPSILON) * norm_gain + norm_bias).astype(jnp.bfloat16)


def contract_last(left, right):
    return lax.dot_general(
        left, right, (((1,), (1,)), ((), ())), preferred_element_type=jnp.float32
    )


def body(states, norm_gain, norm_bias, head_table, seq_lengths, scored_index, targets, slot_mask):
    normed = layer_norm(states, norm_gain, norm_bias)
    local_rows = normed.shape[0]
    devices = lax.axis_size("tensor")
    position = lax.axis_index("tensor")
    first_row = position * local_rows
    scored_count = scored_index.shape[0]
    owned_count = scored_count // devices
    segment = local_rows * devices // seq_lengths.shape[0]
    sequence = scored_index // segment
    seq_iota = jnp.arange(seq_lengths.shape[0], dtype=jnp.int32)
    length_of = jnp.sum(
        jnp.where(sequence[:, None] == seq_iota[None, :], seq_lengths[None, :], 0), axis=1
    )
    live_slot = (slot_mask == 1) & (scored_index % segment < length_of)
    row_iota = jnp.arange(local_rows, dtype=jnp.int32)
    picker = (scored_index[:, None] - first_row == row_iota[None, :]).astype(jnp.bfloat16)
    chosen = lax.psum(jnp.dot(picker, normed, preferred_element_type=jnp.float32), "tensor").astype(
        jnp.bfloat16
    )
    logits = contract_last(chosen, lax.all_gather(head_table, "dp", axis=1, tiled=True))
    vocab_local = head_table.shape[0]
    vocab_iota = jnp.arange(vocab_local, dtype=jnp.int32)
    target_hits = (targets - position * vocab_local)[:, None] == vocab_iota[None, :]
    target_part = jnp.sum(jnp.where(target_hits, logits, 0.0), axis=1)
    local_maxima = jnp.max(logits, axis=1)
    maxima = lax.pmax(local_maxima, "tensor")
    shifted = logits - maxima[:, None]
    weights = jnp.exp(shifted)
    totals, weighted, target_logit = lax.psum(
        (jnp.sum(weights, axis=1), jnp.sum(weights * shifted, axis=1), target_part), "tensor"
    )
    log_total = jnp.log(totals)
    logprob = jnp.where(live_slot, target_logit - maxima - log_total, 0.0)
    entropy = jnp.where(live_slot, log_total - weighted / totals, 0.0)
    offset = position * owned_count
    return (
        lax.dynamic_slice_in_dim(logprob, offset, owned_count),
        lax.dynamic_slice_in_dim(entropy, offset, owned_count),
    )


def solution(mesh):
    return jax.shard_map(
        body,
        mesh=mesh,
        in_specs=(
            P(("dp", "tensor"), None),
            P(),
            P(),
            P("tensor", "dp"),
            P("dp"),
            P("dp"),
            P("dp"),
            P("dp"),
        ),
        out_specs=(P(("dp", "tensor")), P(("dp", "tensor"))),
        check_vma=False,
    )
```

profile of v0, /device:TPU:2, one launch (start us, length us, event | category | flops | bytes accessed | tf_op | source)
XLA Modules:
  0.0 623.1 jit_solution(15719232182898684388)
XLA Ops:
  7.2 0.0 copy-start.1
  7.2 0.0 all-gather.2.cloned.1.call-start
  7.2 0.7 all-gather.2.cloned.1.call-update
  7.9 1.2 convert_reduce_fusion
  9.1 1.3 fusion.3
  10.5 0.7 broadcast_subtract_fusion
  11.1 1.6 fusion.9
  13.4 0.0 copy-done.1
  13.4 308.3 %all-reduce.2 = bf16[256,2048]{1,0:T(8,128)(2,1)S(1)} all-reduce(f32[256,2048]{1,0:T(8,128)S(1)} %fusion.9), channel_id=1, replica_groups=mesh['dp'=8,'tensor'=64] {'tensor'}, use_global_device_ids=true, to_apply=%region_2.3 | all-reduce | flops 524288 | bytes 3145728 | tf_op jit(solution)/shard_map/psum | solution.py:40
  321.7 0.0 all-gather.2.cloned.1.call-done
  321.8 11.9 %fusion.16 = (f32[256]{0:T(256)S(1)}, f32[256,3920]{0,1:T(8,128)}) fusion(bf16[256,2048]{1,0:T(8,128)(2,1)S(1)} %all-reduce.2, bf16[3920,2048]{1,0:T(8,128)(2,1)} %all-gather.2.cloned.1.call-done), kind=kOutput, calls=%fused_computation.35 | convolution fusion | flops 4111421184 | bytes 21120000 | tf_op jit(solution)/shard_map/dot_general | solution.py:18
  333.6 0.0 copy-start
  333.6 0.0 copy-start.2
  333.6 138.0 %pmax.7 = f32[256]{0:T(256)S(1)} all-reduce(f32[256]{0:T(256)S(1)} %get-tuple-element.10), channel_id=1, replica_groups=mesh['dp'=8,'tensor'=64] {'tensor'}, use_global_device_ids=true, to_apply=%region_6.7 | all-reduce | flops 256 | bytes 2048 | tf_op jit(solution)/shard_map/pmax | solution.py:49
  471.6 3.4 fusion
  475.1 139.9 %all-reduce = (f32[256]{0:T(256)S(1)}, f32[256]{0:T(256)S(1)}, f32[256]{0:T(256)S(1)}) all-reduce(f32[256]{0:T(256)S(1)} %get-tuple-element.4, f32[256]{0:T(256)S(1)} %get-tuple-element.3, f32[256]{0:T(256)S(1)} %get-tuple-element.2), channel_id=1, replica_groups=mesh['dp'=8,'tensor'=64] {'tensor'}, use_global_device_ids=true, to_apply=%region_4.5 | all-reduce | flops 768 | bytes 6144 | tf_op jit(solution)/shard_map/psum | solution.py:52
  615.0 0.0 copy-done
  615.0 0.0 copy-done.2
  615.0 0.6 dynamic_slice.7
  615.6 0.6 dynamic_slice.6
  (5 shorter events, 0.0 us)
Async XLA Ops:
  7.2 6.2 %copy-start.1 = (s32[256]{0:T(256)S(1)}, s32[256]{0:T(256)}, u32[]{:S(2)}) copy-start(s32[256]{0:T(256)} %param.14) | copy-start | bytes 3076
  7.2 314.6 %all-gather.2.cloned.1.call-start = ((), (), s32[]{:S(2)}) async-start(), calls=%async_computation | async-start | bytes 18063360 | tf_op jit(solution)/shard_map/all_gather | solution.py:43
  333.6 281.4 %copy-start = (s32[256]{0:T(256)S(1)}, s32[256]{0:T(256)}, u32[]{:S(2)}) copy-start(s32[256]{0:T(256)} %param.13) | copy-start | bytes 3076
  333.6 281.4 %copy-start.2 = (s32[256]{0:T(256)S(1)}, s32[256]{0:T(256)}, u32[]{:S(2)}) copy-start(s32[256]{0:T(256)} %param.15) | copy-start | bytes 3076
Sparse Core Ops, SparseCore 0:
  10.1 99.2 all-gather.1
where the time goes:
time: 623 us
  blocking collectives  586 us (94%)
  between operations  14.7 us (2%)
  matrix products  13.5 us (2%)
  other arithmetic  6.7 us (1%)
    psum x1, blocking collectives, body(): lax.psum(jnp.dot(picker, normed, preferred_element_type=jnp.float32), 'te...  308 us
    psum x1, blocking collectives, body(): lax.psum((jnp.sum(weights, axis=1), jnp.sum(weights * shifted, axis=1), t...  140 us
    pmax x1, blocking collectives, body(): maxima = lax.pmax(local_maxima, 'tensor')  138 us
  transfers between devices with their start and end apart: 1, of which 0 were waited for; matrix products, arithmetic and copies ran while one was open for 1% of the time, Pallas kernels for 0%

commit v1 on v0

v1 whole, which is shorter than its diff:
```python
import jax
import jax.numpy as jnp
from jax import lax
from jax.sharding import PartitionSpec as P

EPSILON = 1e-05


def layer_norm(states, norm_gain, norm_bias):
    values = states.astype(jnp.float32)
    center = jnp.mean(values, axis=1, keepdims=True)
    shifted = values - center
    variance = jnp.mean(shifted * shifted, axis=1, keepdims=True)
    return (shifted * lax.rsqrt(variance + EPSILON) * norm_gain + norm_bias).astype(jnp.bfloat16)


def contract_last(left, right):
    return lax.dot_general(
        left, right, (((1,), (1,)), ((), ())), preferred_element_type=jnp.float32
    )


def body(states, norm_gain, norm_bias, head_table, seq_lengths, scored_index, targets, slot_mask):
    local_rows = states.shape[0]
    devices = lax.axis_size("tensor")
    position = lax.axis_index("tensor")
    first_row = position * local_rows
    scored_count = scored_index.shape[0]
    owned_count = scored_count // devices
    offset = position * owned_count
    width = states.shape[1]

    row_iota = jnp.arange(local_rows, dtype=jnp.int32)
    picker = (scored_index[:, None] - first_row == row_iota[None, :]).astype(jnp.bfloat16)
    picked = jnp.dot(picker, states, preferred_element_type=jnp.float32).astype(jnp.bfloat16)
    arrived = lax.all_to_all(
        picked.reshape(devices, owned_count, width), "tensor", 0, 0, tiled=True
    )
    owned_rows = jnp.sum(arrived.astype(jnp.float32), axis=0)
    owned_normed = layer_norm(owned_rows, norm_gain, norm_bias)
    chosen = lax.all_to_all(
        jnp.broadcast_to(owned_normed[None], (devices, owned_count, width)), "tensor", 0, 0, tiled=True
    ).reshape(scored_count, width)

    logits = contract_last(chosen, lax.all_gather(head_table, "dp", axis=1, tiled=True))
    vocab_local = head_table.shape[0]
    vocab_iota = jnp.arange(vocab_local, dtype=jnp.int32)
    target_hits = (targets - position * vocab_local)[:, None] == vocab_iota[None, :]
    target_part = jnp.sum(jnp.where(target_hits, logits, 0.0), axis=1)
    local_maxima = jnp.max(logits, axis=1)
    shifted = logits - local_maxima[:, None]
    weights = jnp.exp(shifted)
    stats = jnp.stack(
        [local_maxima, jnp.sum(weights, axis=1), jnp.sum(weights * shifted, axis=1), target_part], axis=1
    )
    gathered = lax.all_to_all(stats.reshape(devices, owned_count, 4), "tensor", 0, 0, tiled=True)
    part_max = gathered[:, :, 0]
    maxima = jnp.max(part_max, axis=0)
    gap = part_max - maxima[None, :]
    scale = jnp.exp(gap)
    totals = jnp.sum(scale * gathered[:, :, 1], axis=0)
    weighted = jnp.sum(scale * (gathered[:, :, 2] + gap * gathered[:, :, 1]), axis=0)
    target_logit = jnp.sum(gathered[:, :, 3], axis=0)

    own_index = lax.dynamic_slice_in_dim(scored_index, offset, owned_count)
    own_mask = lax.dynamic_slice_in_dim(slot_mask, offset, owned_count)
    segment = local_rows * devices // seq_lengths.shape[0]
    sequence = own_index // segment
    seq_iota = jnp.arange(seq_lengths.shape[0], dtype=jnp.int32)
    length_of = jnp.sum(
        jnp.where(sequence[:, None] == seq_iota[None, :], seq_lengths[None, :], 0), axis=1
    )
    live_slot = (own_mask == 1) & (own_index % segment < length_of)
    log_total = jnp.log(totals)
    logprob = jnp.where(live_slot, target_logit - maxima - log_total, 0.0)
    entropy = jnp.where(live_slot, log_total - weighted / totals, 0.0)
    return logprob, entropy


def solution(mesh):
    return jax.shard_map(
        body,
        mesh=mesh,
        in_specs=(
            P(("dp", "tensor"), None),
            P(),
            P(),
            P("tensor", "dp"),
            P("dp"),
            P("dp"),
            P("dp"),
            P("dp"),
        ),
        out_specs=(P(("dp", "tensor")), P(("dp", "tensor"))),
        check_vma=False,
    )
```

time: 623 us -> 195 us (0.31)
  the two profiles are of different devices: /device:TPU:2 before, /device:TPU:1 now
where the time goes in v1:
time: 195 us; the launch traced here: 192 us
  blocking collectives  70.5 us (36%)
  waiting for transfers between devices  66 us (34%)
  starting transfers between devices  17.6 us (9%)
  between operations  14.9 us (8%)
  matrix products  12.3 us (6%)
  other arithmetic  7.12 us (4%)
  local copies, waits for them, and re-layouts  3.54 us (2%)
    all_to_all x1, blocking collectives, body(): lax.all_to_all(picked.reshape(devices, owned_count, width), 'tensor', 0,...  70.5 us
    all_to_all x1, waiting for transfers between devices, body(): lax.all_to_all(jnp.broadcast_to(owned_normed[None], (devices, owned_count...  51 us
    all_to_all x1, waiting for transfers between devices, body(): lax.all_to_all(stats.reshape(devices, owned_count, 4), 'tensor', 0, 0, ti...  14.3 us
    dot_general x1, matrix products, contract_last(): lax.dot_general(left, right, (((1,), (1,)), ((), ())), preferred_element_...  11.9 us
    all_to_all x1, starting transfers between devices, body(): lax.all_to_all(jnp.broadcast_to(owned_normed[None], (devices, owned_count...  9.02 us
    all_to_all x1, starting transfers between devices, body(): lax.all_to_all(stats.reshape(devices, owned_count, 4), 'tensor', 0, 0, ti...  8.58 us
  transfers between devices with their start and end apart: 3, of which 2 were waited for; matrix products, arithmetic and copies ran while one was open for 3% of the time, Pallas kernels for 0%

profile of v1, /device:TPU:1, one launch (start us, length us, event | category | flops | bytes accessed | tf_op | source)
XLA Modules:
  0.0 192.0 jit_solution(10826240875492589096)
XLA Ops:
  7.2 0.0 copy-start
  7.2 0.0 all-gather.2.cloned.1.call-start
  7.2 0.7 all-gather.2.cloned.1.call-update
  7.9 0.7 broadcast_subtract_fusion.1
  8.6 0.5 convolution_convert_fusion
  9.1 0.0 copy-start.4
  9.1 0.4 reshape.104
  9.5 70.5 %all_to_all.15 = bf16[64,4,2048]{2,1,0:T(4,128)(2,1)S(1)} all-to-all(bf16[64,4,2048]{2,1,0:T(4,128)(2,1)S(1)} %reshape.104), channel_id=1, replica_groups=mesh['dp'=8,'tensor'=64] {'tensor'}, dimensions={0} | all-to-all | bytes 2097152 | tf_op jit(solution)/shard_map/all_to_all | solution.py:36
  80.1 1.2 convert_reduce_fusion
  81.3 0.2 multiply_reduce_fusion
  81.5 0.1 add_convert_fusion
  81.6 1.5 broadcast_in_dim.20
  83.1 9.0 %all-to-all-start.1 = ((bf16[64,4,2048]{2,1,0:T(4,128)(2,1)}), bf16[64,4,2048]{2,1,0:T(4,128)(2,1)S(1)}, u32[]{:S(2)}, u32[]{:S(2)}) async-start(bf16[64,4,2048]{2,1,0:T(4,128)(2,1)} %broadcast_in_dim.20), calls=%async_computation.1 | async-start | bytes 2097152 | tf_op jit(solution)/shard_map/all_to_all | solution.py:41
  92.1 51.0 %all-to-all-done.1 = bf16[64,4,2048]{2,1,0:T(4,128)(2,1)S(1)} async-done(((bf16[64,4,2048]{2,1,0:T(4,128)(2,1)}), bf16[64,4,2048]{2,1,0:T(4,128)(2,1)S(1)}, u32[]{:S(2)}, u32[]{:S(2)}) %all-to-all-start.1) | async-done | bytes 1048608 | tf_op jit(solution)/shard_map/all_to_all | solution.py:41
  143.1 0.3 reshape.105
  143.4 0.0 all-gather.2.cloned.1.call-done
  143.4 11.9 %fusion.6 = (f32[256]{0:T(256)S(1)}, f32[256,3920]{0,1:T(8,128)}) fusion(bf16[256,2048]{1,0:T(8,128)(2,1)S(1)} %reshape.105, bf16[3920,2048]{1,0:T(8,128)(2,1)} %all-gather.2.cloned.1.call-done), kind=kOutput, calls=%fused_computation.36 | convolution fusion | flops 4111421184 | bytes 21120000 | tf_op jit(solution)/shard_map/dot_general | solution.py:18
  155.3 0.1 stack.15
  155.4 3.4 %exponential_reduce_fusion = (f32[256]{0:T(256)S(1)}, f32[256]{0:T(256)S(1)}, f32[256]{0:T(256)S(1)}) fusion(f32[256,3920]{0,1:T(8,128)} %get-tuple-element.17, f32[256]{0:T(256)S(1)} %get-tuple-element.16, s32[256]{0:T(256)S(1)} %broadcast_subtract_fusion), kind=kLoop, calls=%fused_computation.1 | loop fusion | flops 7023872 | bytes 4019200 | tf_op jit(solution)/shard_map/reduce_sum | solution.py:54
  158.8 0.1 stack.16
  158.9 0.1 stack.17
  159.0 0.1 stack.18
  159.2 0.7 copy.22
  159.9 8.6 %all-to-all-start.2 = ((f32[64,4,4]{1,2,0:T(4,128)}), f32[64,4,4]{1,2,0:T(4,128)S(1)}, u32[]{:S(2)}, u32[]{:S(2)}) async-start(f32[64,4,4]{1,2,0:T(4,128)} %copy.22), calls=%async_computation.2 | async-start | bytes 262144 | tf_op jit(solution)/shard_map/all_to_all | solution.py:56
  169.1 14.3 %all-to-all-done.2 = f32[64,4,4]{1,2,0:T(4,128)S(1)} async-done(((f32[64,4,4]{1,2,0:T(4,128)}), f32[64,4,4]{1,2,0:T(4,128)S(1)}, u32[]{:S(2)}, u32[]{:S(2)}) %all-to-all-start.2) | async-done | bytes 4128 | tf_op jit(solution)/shard_map/all_to_all | solution.py:56
  183.5 0.1 slice_reduce_fusion.1
  183.6 0.1 copy.25
  183.7 0.1 copy.26
  183.7 0.1 copy.27
  183.8 0.2 fusion.3
  184.1 0.6 subtract_select_fusion
  184.7 0.5 subtract_select_fusion.1
  (14 shorter events, 0.1 us)
Async XLA Ops:
  7.2 1.5 copy-start
  7.2 74.3 %copy-start.1 = (f32[2048]{0:T(1024)S(1)}, f32[2048]{0:T(1024)}, u32[]{:S(2)}) copy-start(f32[2048]{0:T(1024)} %param.10) | copy-start | bytes 24580
  7.2 74.3 %copy-start.2 = (f32[2048]{0:T(1024)S(1)}, f32[2048]{0:T(1024)}, u32[]{:S(2)}) copy-start(f32[2048]{0:T(1024)} %param.9) | copy-start | bytes 24580
  7.2 136.2 %all-gather.2.cloned.1.call-start = ((), (), s32[]{:S(2)}) async-start(), calls=%async_computation.3 | async-start | bytes 18063360 | tf_op jit(solution)/shard_map/all_gather | solution.py:45
  9.1 83.0 %copy-start.4 = (s32[256]{0:T(256)S(1)}, s32[256]{0:T(256)}, u32[]{:S(2)}) copy-start(s32[256]{0:T(256)} %param.14) | copy-start | bytes 3076
  83.1 60.0 %all-to-all-start.1 = ((bf16[64,4,2048]{2,1,0:T(4,128)(2,1)}), bf16[64,4,2048]{2,1,0:T(4,128)(2,1)S(1)}, u32[]{:S(2)}, u32[]{:S(2)}) async-start(bf16[64,4,2048]{2,1,0:T(4,128)(2,1)} %broadcast_in_dim.20), calls=%async_computation.1 | async-start | bytes 2097152 | tf_op jit(solution)/shard_map/all_to_all | solution.py:41
  155.3 28.8 %copy-start.3 = (s32[256]{0:T(256)S(1)}, s32[256]{0:T(256)}, u32[]{:S(2)}) copy-start(s32[256]{0:T(256)} %param.13) | copy-start | bytes 3076
  155.3 28.8 %copy-start.5 = (s32[256]{0:T(256)S(1)}, s32[256]{0:T(256)}, u32[]{:S(2)}) copy-start(s32[256]{0:T(256)} %param.15) | copy-start | bytes 3076
  159.9 23.6 %all-to-all-start.2 = ((f32[64,4,4]{1,2,0:T(4,128)}), f32[64,4,4]{1,2,0:T(4,128)S(1)}, u32[]{:S(2)}, u32[]{:S(2)}) async-start(f32[64,4,4]{1,2,0:T(4,128)} %copy.22), calls=%async_computation.2 | async-start | bytes 262144 | tf_op jit(solution)/shard_map/all_to_all | solution.py:56
Sparse Core Ops, SparseCore 0:
  10.2 100.5 all-gather.1

commit v2 on v1

--- a/solution.py
+++ b/solution.py
@@ -1,9 +1,10 @@
 import jax
 import jax.numpy as jnp
 from jax import lax
-from jax.sharding import PartitionSpec as P
+from jax.sharding import Mesh, PartitionSpec as P
 
 EPSILON = 1e-05
+TENSOR = ("tz", "ty")
 
 
 def layer_norm(states, norm_gain, norm_bias):
@@ -22,8 +23,8 @@
 
 def body(states, norm_gain, norm_bias, head_table, seq_lengths, scored_index, targets, slot_mask):
     local_rows = states.shape[0]
-    devices = lax.axis_size("tensor")
-    position = lax.axis_index("tensor")
+    devices = lax.axis_size(TENSOR)
+    position = lax.axis_index(TENSOR)
     first_row = position * local_rows
     scored_count = scored_index.shape[0]
     owned_count = scored_count // devices
@@ -33,13 +34,15 @@
     row_iota = jnp.arange(local_rows, dtype=jnp.int32)
     picker = (scored_index[:, None] - first_row == row_iota[None, :]).astype(jnp.bfloat16)
     picked = jnp.dot(picker, states, preferred_element_type=jnp.float32).astype(jnp.bfloat16)
-    arrived = lax.all_to_all(
-        picked.reshape(devices, owned_count, width), "tensor", 0, 0, tiled=True
-    )
+    ring = lax.axis_size("ty")
+    by_y = picked.reshape(devices // ring, ring, owned_count, width).transpose(1, 0, 2, 3)
+    near = lax.all_to_all(by_y, "ty", 0, 0, tiled=True)
+    near = jnp.sum(near.astype(jnp.float32), axis=0).astype(jnp.bfloat16)
+    arrived = lax.all_to_all(near, "tz", 0, 0, tiled=True)
     owned_rows = jnp.sum(arrived.astype(jnp.float32), axis=0)
     owned_normed = layer_norm(owned_rows, norm_gain, norm_bias)
     chosen = lax.all_to_all(
-        jnp.broadcast_to(owned_normed[None], (devices, owned_count, width)), "tensor", 0, 0, tiled=True
+        jnp.broadcast_to(owned_normed[None], (devices, owned_count, width)), TENSOR, 0, 0, tiled=True
     ).reshape(scored_count, width)
 
     logits = contract_last(chosen, lax.all_gather(head_table, "dp", axis=1, tiled=True))
@@ -53,7 +56,7 @@
     stats = jnp.stack(
         [local_maxima, jnp.sum(weights, axis=1), jnp.sum(weights * shifted, axis=1), target_part], axis=1
     )
-    gathered = lax.all_to_all(stats.reshape(devices, owned_count, 4), "tensor", 0, 0, tiled=True)
+    gathered = lax.all_to_all(stats.reshape(devices, owned_count, 4), TENSOR, 0, 0, tiled=True)
     part_max = gathered[:, :, 0]
     maxima = jnp.max(part_max, axis=0)
     gap = part_max - maxima[None, :]
@@ -77,20 +80,28 @@
     return logprob, entropy
 
 
+def split_mesh(mesh):
+    grid = mesh.devices
+    first = grid[0]
+    coords = [getattr(d, "coords", None) for d in first]
+    ring = len({c[1] for c in coords}) if all(c is not None for c in coords) else 1
+    return Mesh(grid.reshape(grid.shape[0], grid.shape[1] // ring, ring), ("dp", "tz", "ty"))
+
+
 def solution(mesh):
     return jax.shard_map(
         body,
-        mesh=mesh,
+        mesh=split_mesh(mesh),
         in_specs=(
-            P(("dp", "tensor"), None),
+            P(("dp", "tz", "ty"), None),
             P(),
             P(),
-            P("tensor", "dp"),
+            P(("tz", "ty"), "dp"),
             P("dp"),
             P("dp"),
             P("dp"),
             P("dp"),
         ),
-        out_specs=(P(("dp", "tensor")), P(("dp", "tensor"))),
+        out_specs=(P(("dp", "tz", "ty")), P(("dp", "tz", "ty"))),
         check_vma=False,
     )

time: 195 us -> 173 us (0.89)
  blocking collectives: 70.5 us -> 46.5 us
  starting transfers between devices: 17.6 us -> 21.3 us
    all_to_all x1 -> x2, blocking collectives: 70.5 us -> 46.5 us  [the longest x1 31 us: body(): arrived = lax.all_to_all(near, 'tz', 0, 0, tiled=True)]
    all_to_all x1, starting transfers between devices: 9.02 us -> 11.2 us  [body(): lax.all_to_all(jnp.broadcast_to(owned_normed[None], (devices, owned_count...]
where the time goes in v2:
time: 173 us; the launch traced here: 170 us
  waiting for transfers between devices  64.3 us (37%)
  blocking collectives  46.5 us (27%)
  starting transfers between devices  21.3 us (12%)
  between operations  14.9 us (9%)
  matrix products  12.3 us (7%)
  other arithmetic  7.06 us (4%)
  local copies, waits for them, and re-layouts  4 us (2%)
    all_to_all x1, waiting for transfers between devices, body(): lax.all_to_all(jnp.broadcast_to(owned_normed[None], (devices, owned_count...  49.2 us
    all_to_all x1, blocking collectives, body(): arrived = lax.all_to_all(near, 'tz', 0, 0, tiled=True)  31 us
    all_to_all x1, blocking collectives, body(): near = lax.all_to_all(by_y, 'ty', 0, 0, tiled=True)  15.5 us
    all_to_all x1, waiting for transfers between devices, body(): lax.all_to_all(stats.reshape(devices, owned_count, 4), TENSOR, 0, 0, tile...  14.3 us
    dot_general x1, matrix products, contract_last(): lax.dot_general(left, right, (((1,), (1,)), ((), ())), preferred_element_...  11.9 us
    all_to_all x1, starting transfers between devices, body(): lax.all_to_all(jnp.broadcast_to(owned_normed[None], (devices, owned_count...  11.2 us
    all_to_all x1, starting transfers between devices, body(): lax.all_to_all(stats.reshape(devices, owned_count, 4), TENSOR, 0, 0, tile...  9.99 us
  transfers between devices with their start and end apart: 3, of which 2 were waited for; matrix products, arithmetic and copies ran while one was open for 3% of the time, Pallas kernels for 0%

profile of v2, /device:TPU:1, one launch (start us, length us, event | category | flops | bytes accessed | tf_op | source)
XLA Modules:
  0.0 170.3 jit_solution(16491705563330118771)
XLA Ops:
  7.2 0.0 all-gather.2.cloned.1.call-start
  7.2 0.7 all-gather.2.cloned.1.call-update
  7.9 0.7 broadcast_subtract_fusion.1
  8.6 0.5 convolution_convert_fusion
  9.1 0.4 reshape.104
  9.5 0.5 copy.47
  10.0 15.5 %all_to_all.20 = bf16[4,16,4,2048]{3,2,1,0:T(4,128)(2,1)S(1)} all-to-all(bf16[4,16,4,2048]{3,2,1,0:T(4,128)(2,1)S(1)} %bitcast.31), channel_id=1, replica_groups=mesh['dp'=8,'tz'=16,'ty'=4] {'ty'}, dimensions={0} | all-to-all | bytes 2097152 | tf_op jit(solution)/shard_map/all_to_all | solution.py:39
  25.5 0.7 reduce_sum.97
  26.2 31.0 %all_to_all.21 = bf16[16,4,2048]{2,1,0:T(4,128)(2,1)S(1)} all-to-all(bf16[16,4,2048]{2,1,0:T(4,128)(2,1)S(1)} %reduce_sum.97), channel_id=1, replica_groups=mesh['dp'=8,'tz'=16,'ty'=4] {'tz'}, dimensions={0} | all-to-all | bytes 524288 | tf_op jit(solution)/shard_map/all_to_all | solution.py:41
  57.3 0.4 convert_reduce_fusion
  57.7 0.2 multiply_reduce_fusion
  57.9 0.1 add_convert_fusion
  58.0 1.5 broadcast_in_dim.20
  59.5 11.2 %all-to-all-start.2 = ((bf16[64,4,2048]{2,1,0:T(4,128)(2,1)}), bf16[64,4,2048]{2,1,0:T(4,128)(2,1)S(1)}, u32[]{:S(2)}, u32[]{:S(2)}) async-start(bf16[64,4,2048]{2,1,0:T(4,128)(2,1)} %broadcast_in_dim.20), calls=%async_computation.2 | async-start | bytes 2097152 | tf_op jit(solution)/shard_map/all_to_all | solution.py:44
  70.7 49.2 %all-to-all-done.2 = bf16[64,4,2048]{2,1,0:T(4,128)(2,1)S(1)} async-done(((bf16[64,4,2048]{2,1,0:T(4,128)(2,1)}), bf16[64,4,2048]{2,1,0:T(4,128)(2,1)S(1)}, u32[]{:S(2)}, u32[]{:S(2)}) %all-to-all-start.2) | async-done | bytes 1048608 | tf_op jit(solution)/shard_map/all_to_all | solution.py:44
  120.0 0.3 reshape.105
  120.2 11.9 %fusion.6 = (f32[256]{0:T(256)S(1)}, f32[256,3920]{0,1:T(8,128)}) fusion(bf16[256,2048]{1,0:T(8,128)(2,1)S(1)} %reshape.105, bf16[3920,2048]{1,0:T(8,128)(2,1)} %all-gather.2.cloned.1.call-done), kind=kOutput, calls=%fused_computation.37 | convolution fusion | flops 4111421184 | bytes 21120000 | tf_op jit(solution)/shard_map/dot_general | solution.py:19
  132.1 0.1 stack.15
  132.2 3.4 %exponential_reduce_fusion = (f32[256]{0:T(256)S(1)}, f32[256]{0:T(256)S(1)}, f32[256]{0:T(256)S(1)}) fusion(f32[256,3920]{0,1:T(8,128)} %get-tuple-element.17, f32[256]{0:T(256)S(1)} %get-tuple-element.16, s32[256]{0:T(256)S(1)} %broadcast_subtract_fusion), kind=kLoop, calls=%fused_computation.1 | loop fusion | flops 7023872 | bytes 4019200 | tf_op jit(solution)/shard_map/reduce_sum | solution.py:57
  135.7 0.1 stack.16
  135.8 0.1 stack.17
  135.9 0.1 stack.18
  136.0 0.7 copy.37
  136.7 10.0 %all-to-all-start.3 = ((f32[64,4,4]{1,2,0:T(4,128)}), f32[64,4,4]{1,2,0:T(4,128)S(1)}, u32[]{:S(2)}, u32[]{:S(2)}) async-start(f32[64,4,4]{1,2,0:T(4,128)} %copy.37), calls=%async_computation.3 | async-start | bytes 262144 | tf_op jit(solution)/shard_map/all_to_all | solution.py:59
  147.4 14.3 %all-to-all-done.3 = f32[64,4,4]{1,2,0:T(4,128)S(1)} async-done(((f32[64,4,4]{1,2,0:T(4,128)}), f32[64,4,4]{1,2,0:T(4,128)S(1)}, u32[]{:S(2)}, u32[]{:S(2)}) %all-to-all-start.3) | async-done | bytes 4128 | tf_op jit(solution)/shard_map/all_to_all | solution.py:59
  161.7 0.1 slice_reduce_fusion.1
  161.9 0.1 copy.40
  161.9 0.1 copy.41
  162.0 0.1 copy.42
  162.1 0.2 fusion.3
  162.3 0.6 subtract_select_fusion
  162.9 0.5 subtract_select_fusion.1
  (17 shorter events, 0.1 us)
Async XLA Ops:
  7.2 1.4 copy-start
  7.2 113.1 %all-gather.2.cloned.1.call-start = ((), (), s32[]{:S(2)}) async-start(), calls=%async_computation.4 | async-start | bytes 18063360 | tf_op jit(solution)/shard_map/all_gather | solution.py:48
  9.1 48.8 %copy-start.1 = (f32[2048]{0:T(1024)S(1)}, f32[2048]{0:T(1024)}, u32[]{:S(2)}) copy-start(f32[2048]{0:T(1024)} %param.10) | copy-start | bytes 24580
  9.1 48.8 %copy-start.2 = (f32[2048]{0:T(1024)S(1)}, f32[2048]{0:T(1024)}, u32[]{:S(2)}) copy-start(f32[2048]{0:T(1024)} %param.9) | copy-start | bytes 24580
  10.0 60.7 %copy-start.4 = (s32[256]{0:T(256)S(1)}, s32[256]{0:T(256)}, u32[]{:S(2)}) copy-start(s32[256]{0:T(256)} %param.14) | copy-start | bytes 3076
  59.5 60.5 %all-to-all-start.2 = ((bf16[64,4,2048]{2,1,0:T(4,128)(2,1)}), bf16[64,4,2048]{2,1,0:T(4,128)(2,1)S(1)}, u32[]{:S(2)}, u32[]{:S(2)}) async-start(bf16[64,4,2048]{2,1,0:T(4,128)(2,1)} %broadcast_in_dim.20), calls=%async_computation.2 | async-start | bytes 2097152 | tf_op jit(solution)/shard_map/all_to_all | solution.py:44
  132.1 30.2 %copy-start.3 = (s32[256]{0:T(256)S(1)}, s32[256]{0:T(256)}, u32[]{:S(2)}) copy-start(s32[256]{0:T(256)} %param.13) | copy-start | bytes 3076
  132.1 30.2 %copy-start.5 = (s32[256]{0:T(256)S(1)}, s32[256]{0:T(256)}, u32[]{:S(2)}) copy-start(s32[256]{0:T(256)} %param.15) | copy-start | bytes 3076
  136.7 25.0 %all-to-all-start.3 = ((f32[64,4,4]{1,2,0:T(4,128)}), f32[64,4,4]{1,2,0:T(4,128)S(1)}, u32[]{:S(2)}, u32[]{:S(2)}) async-start(f32[64,4,4]{1,2,0:T(4,128)} %copy.37), calls=%async_computation.3 | async-start | bytes 262144 | tf_op jit(solution)/shard_map/all_to_all | solution.py:59
Sparse Core Ops, SparseCore 0:
  10.1 100.6 all-gather.1

commit v3 on v2

--- a/solution.py
+++ b/solution.py
@@ -41,9 +41,13 @@
     arrived = lax.all_to_all(near, "tz", 0, 0, tiled=True)
     owned_rows = jnp.sum(arrived.astype(jnp.float32), axis=0)
     owned_normed = layer_norm(owned_rows, norm_gain, norm_bias)
-    chosen = lax.all_to_all(
-        jnp.broadcast_to(owned_normed[None], (devices, owned_count, width)), TENSOR, 0, 0, tiled=True
-    ).reshape(scored_count, width)
+    along_z = lax.all_to_all(
+        jnp.broadcast_to(owned_normed[None], (devices // ring, owned_count, width)), "tz", 0, 0, tiled=True
+    )
+    along_y = lax.all_to_all(
+        jnp.broadcast_to(along_z[None], (ring, devices // ring, owned_count, width)), "ty", 0, 0, tiled=True
+    )
+    chosen = along_y.transpose(1, 0, 2, 3).reshape(scored_count, width)
 
     logits = contract_last(chosen, lax.all_gather(head_table, "dp", axis=1, tiled=True))
     vocab_local = head_table.shape[0]

time: 173 us -> 169 us (0.977)
  waiting for transfers between devices: 64.3 us -> 40.1 us
  blocking collectives: 46.5 us -> 68.8 us
  starting transfers between devices: 21.3 us -> 18.9 us
    all_to_all x1, waiting for transfers between devices: 49.2 us -> 9.69 us  [body(): lax.all_to_all(jnp.broadcast_to(along_z[None], (ring, devices // ring, ow...]
    all_to_all x0 -> x1, blocking collectives: none -> 22.3 us  [body(): lax.all_to_all(jnp.broadcast_to(owned_normed[None], (devices // ring, own...]
    all_gather x1, waiting for transfers between devices: 0.02 us -> 14.9 us  [body(): lax.all_gather(head_table, 'dp', axis=1, tiled=True)]
    all_to_all x1, starting transfers between devices: 11.2 us -> 3.56 us  [body(): lax.all_to_all(jnp.broadcast_to(along_z[None], (ring, devices // ring, ow...]
    all_to_all x1, starting transfers between devices: 9.99 us -> 15.3 us  [body(): lax.all_to_all(stats.reshape(devices, owned_count, 4), TENSOR, 0, 0, tile...]
  transfers between devices with their start and end apart: 3 -> 3, of which waited for: 2 -> 3; matrix products, arithmetic and copies ran while one was open for 3% -> 3% of each run, Pallas kernels for 0% -> 0%
where the time goes in v3:
time: 169 us; the launch traced here: 167 us
  blocking collectives  68.8 us (41%)
  waiting for transfers between devices  40.1 us (24%)
  starting transfers between devices  18.9 us (11%)
  between operations  14.9 us (9%)
  matrix products  12.3 us (7%)
  other arithmetic  7.06 us (4%)
  local copies, waits for them, and re-layouts  4.58 us (3%)
    all_to_all x1, blocking collectives, body(): arrived = lax.all_to_all(near, 'tz', 0, 0, tiled=True)  31 us
    all_to_all x1, blocking collectives, body(): lax.all_to_all(jnp.broadcast_to(owned_normed[None], (devices // ring, own...  22.3 us
    all_to_all x1, blocking collectives, body(): near = lax.all_to_all(by_y, 'ty', 0, 0, tiled=True)  15.5 us
    all_to_all x1, starting transfers between devices, body(): lax.all_to_all(stats.reshape(devices, owned_count, 4), TENSOR, 0, 0, tile...  15.3 us
    all_gather x1, waiting for transfers between devices, body(): lax.all_gather(head_table, 'dp', axis=1, tiled=True)  14.9 us
    all_to_all x1, waiting for transfers between devices, body(): lax.all_to_all(stats.reshape(devices, owned_count, 4), TENSOR, 0, 0, tile...  14.8 us
    dot_general x1, matrix products, contract_last(): lax.dot_general(left, right, (((1,), (1,)), ((), ())), preferred_element_...  11.9 us
    all_to_all x1, waiting for transfers between devices, body(): lax.all_to_all(jnp.broadcast_to(along_z[None], (ring, devices // ring, ow...  9.69 us
  transfers between devices with their start and end apart: 3, of which 3 were waited for; matrix products, arithmetic and copies ran while one was open for 3% of the time, Pallas kernels for 0%

profile of v3, /device:TPU:1, one launch (start us, length us, event | category | flops | bytes accessed | tf_op | source)
XLA Modules:
  0.0 166.6 jit_solution(15493609864118284979)
XLA Ops:
  7.2 0.7 all-gather.2.cloned.1.call-update
  7.9 0.7 broadcast_subtract_fusion.1
  8.6 0.5 convolution_convert_fusion
  9.1 0.4 reshape.105
  9.5 0.5 copy.51
  10.0 15.5 %all_to_all.25 = bf16[4,16,4,2048]{3,2,1,0:T(4,128)(2,1)S(1)} all-to-all(bf16[4,16,4,2048]{3,2,1,0:T(4,128)(2,1)S(1)} %bitcast.33), channel_id=1, replica_groups=mesh['dp'=8,'tz'=16,'ty'=4] {'ty'}, dimensions={0} | all-to-all | bytes 2097152 | tf_op jit(solution)/shard_map/all_to_all | solution.py:39
  25.5 0.7 reduce_sum.97
  26.2 31.0 %all_to_all.26 = bf16[16,4,2048]{2,1,0:T(4,128)(2,1)S(1)} all-to-all(bf16[16,4,2048]{2,1,0:T(4,128)(2,1)S(1)} %reduce_sum.97), channel_id=1, replica_groups=mesh['dp'=8,'tz'=16,'ty'=4] {'tz'}, dimensions={0} | all-to-all | bytes 524288 | tf_op jit(solution)/shard_map/all_to_all | solution.py:41
  57.3 0.4 convert_reduce_fusion
  57.7 0.2 multiply_reduce_fusion
  57.9 0.1 add_convert_fusion
  58.0 0.1 broadcast_in_dim.22
  58.1 22.3 %all_to_all.27 = bf16[16,4,2048]{2,1,0:T(4,128)(2,1)S(1)} all-to-all(bf16[16,4,2048]{2,1,0:T(4,128)(2,1)S(1)} %broadcast_in_dim.22), channel_id=1, replica_groups=mesh['dp'=8,'tz'=16,'ty'=4] {'tz'}, dimensions={0} | all-to-all | bytes 524288 | tf_op jit(solution)/shard_map/all_to_all | solution.py:44
  80.4 1.5 broadcast_in_dim.23
  81.9 3.6 %all-to-all-start.3 = ((bf16[4,16,4,2048]{3,2,1,0:T(4,128)(2,1)}), bf16[4,16,4,2048]{3,2,1,0:T(4,128)(2,1)S(1)}, u32[]{:S(2)}, u32[]{:S(2)}) async-start(bf16[4,16,4,2048]{3,2,1,0:T(4,128)(2,1)} %broadcast_in_dim.23), calls=%async_computation.3 | async-start | bytes 2097152 | tf_op jit(solution)/shard_map/all_to_all | solution.py:47
  85.5 9.7 %all-to-all-done.3 = bf16[4,16,4,2048]{3,2,1,0:T(4,128)(2,1)S(1)} async-done(((bf16[4,16,4,2048]{3,2,1,0:T(4,128)(2,1)}), bf16[4,16,4,2048]{3,2,1,0:T(4,128)(2,1)S(1)}, u32[]{:S(2)}, u32[]{:S(2)}) %all-to-all-start.3) | async-done | bytes 1048608 | tf_op jit(solution)/shard_map/all_to_all | solution.py:47
  95.2 0.5 copy.40
  95.6 0.3 reshape.106
  95.9 14.9 %all-gather.2.cloned.1.call-done = bf16[3920,2048]{1,0:T(8,128)(2,1)} async-done(((bf16[3920,256]{1,0:T(8,128)(2,1)}), bf16[3920,2048]{1,0:T(8,128)(2,1)}) %all-gather.2.cloned.1.call-update) | async-done | bytes 16056336 | tf_op jit(solution)/shard_map/all_gather | solution.py:52
  110.8 11.9 %fusion.6 = (f32[256]{0:T(256)S(1)}, f32[256,3920]{0,1:T(8,128)}) fusion(bf16[256,2048]{1,0:T(8,128)(2,1)S(1)} %reshape.106, bf16[3920,2048]{1,0:T(8,128)(2,1)} %all-gather.2.cloned.1.call-done), kind=kOutput, calls=%fused_computation.37 | convolution fusion | flops 4111421184 | bytes 21120000 | tf_op jit(solution)/shard_map/dot_general | solution.py:19
  122.7 0.1 stack.15
  122.8 3.4 %exponential_reduce_fusion = (f32[256]{0:T(256)S(1)}, f32[256]{0:T(256)S(1)}, f32[256]{0:T(256)S(1)}) fusion(f32[256,3920]{0,1:T(8,128)} %get-tuple-element.17, f32[256]{0:T(256)S(1)} %get-tuple-element.16, s32[256]{0:T(256)S(1)} %broadcast_subtract_fusion), kind=kLoop, calls=%fused_computation.1 | loop fusion | flops 7023872 | bytes 4019200 | tf_op jit(solution)/shard_map/reduce_sum | solution.py:61
  126.2 0.1 stack.16
  126.3 0.1 stack.17
  126.4 0.1 stack.18
  126.6 0.7 copy.41
  127.3 15.3 %all-to-all-start.4 = ((f32[64,4,4]{1,2,0:T(4,128)}), f32[64,4,4]{1,2,0:T(4,128)S(1)}, u32[]{:S(2)}, u32[]{:S(2)}) async-start(f32[64,4,4]{1,2,0:T(4,128)} %copy.41), calls=%async_computation.4 | async-start | bytes 262144 | tf_op jit(solution)/shard_map/all_to_all | solution.py:63
  143.2 14.8 %all-to-all-done.4 = f32[64,4,4]{1,2,0:T(4,128)S(1)} async-done(((f32[64,4,4]{1,2,0:T(4,128)}), f32[64,4,4]{1,2,0:T(4,128)S(1)}, u32[]{:S(2)}, u32[]{:S(2)}) %all-to-all-start.4) | async-done | bytes 4128 | tf_op jit(solution)/shard_map/all_to_all | solution.py:63
  158.1 0.1 slice_reduce_fusion.1
  158.4 0.2 fusion.3
  158.6 0.6 subtract_select_fusion
  159.2 0.5 subtract_select_fusion.1
  (20 shorter events, 0.3 us)
Async XLA Ops:
  7.2 1.4 copy-start
  7.2 103.6 %all-gather.2.cloned.1.call-start = ((), (), s32[]{:S(2)}) async-start(), calls=%async_computation.5 | async-start | bytes 18063360 | tf_op jit(solution)/shard_map/all_gather | solution.py:52
  9.1 48.8 %copy-start.1 = (f32[2048]{0:T(1024)S(1)}, f32[2048]{0:T(1024)}, u32[]{:S(2)}) copy-start(f32[2048]{0:T(1024)} %param.10) | copy-start | bytes 24580
  9.1 48.8 %copy-start.2 = (f32[2048]{0:T(1024)S(1)}, f32[2048]{0:T(1024)}, u32[]{:S(2)}) copy-start(f32[2048]{0:T(1024)} %param.9) | copy-start | bytes 24580
  10.0 75.5 %copy-start.4 = (s32[256]{0:T(256)S(1)}, s32[256]{0:T(256)}, u32[]{:S(2)}) copy-start(s32[256]{0:T(256)} %param.14) | copy-start | bytes 3076
  81.9 13.3 %all-to-all-start.3 = ((bf16[4,16,4,2048]{3,2,1,0:T(4,128)(2,1)}), bf16[4,16,4,2048]{3,2,1,0:T(4,128)(2,1)S(1)}, u32[]{:S(2)}, u32[]{:S(2)}) async-start(bf16[4,16,4,2048]{3,2,1,0:T(4,128)(2,1)} %broadcast_in_dim.23), calls=%async_computation.3 | async-start | bytes 2097152 | tf_op jit(solution)/shard_map/all_to_all | solution.py:47
  122.7 36.0 %copy-start.3 = (s32[256]{0:T(256)S(1)}, s32[256]{0:T(256)}, u32[]{:S(2)}) copy-start(s32[256]{0:T(256)} %param.13) | copy-start | bytes 3076
  122.7 36.0 %copy-start.5 = (s32[256]{0:T(256)S(1)}, s32[256]{0:T(256)}, u32[]{:S(2)}) copy-start(s32[256]{0:T(256)} %param.15) | copy-start | bytes 3076
  127.3 30.8 %all-to-all-start.4 = ((f32[64,4,4]{1,2,0:T(4,128)}), f32[64,4,4]{1,2,0:T(4,128)S(1)}, u32[]{:S(2)}, u32[]{:S(2)}) async-start(f32[64,4,4]{1,2,0:T(4,128)} %copy.41), calls=%async_computation.4 | async-start | bytes 262144 | tf_op jit(solution)/shard_map/all_to_all | solution.py:63
Sparse Core Ops, SparseCore 0:
  10.1 100.6 all-gather.1

commit v4 on v3

--- a/solution.py
+++ b/solution.py
@@ -49,18 +49,31 @@
     )
     chosen = along_y.transpose(1, 0, 2, 3).reshape(scored_count, width)
 
-    logits = contract_last(chosen, lax.all_gather(head_table, "dp", axis=1, tiled=True))
     vocab_local = head_table.shape[0]
-    vocab_iota = jnp.arange(vocab_local, dtype=jnp.int32)
-    target_hits = (targets - position * vocab_local)[:, None] == vocab_iota[None, :]
-    target_part = jnp.sum(jnp.where(target_hits, logits, 0.0), axis=1)
-    local_maxima = jnp.max(logits, axis=1)
-    shifted = logits - local_maxima[:, None]
-    weights = jnp.exp(shifted)
-    stats = jnp.stack(
-        [local_maxima, jnp.sum(weights, axis=1), jnp.sum(weights * shifted, axis=1), target_part], axis=1
-    )
-    gathered = lax.all_to_all(stats.reshape(devices, owned_count, 4), TENSOR, 0, 0, tiled=True)
+    split = (vocab_local // 32) * 16
+    local_target = targets - position * vocab_local
+    parts = []
+    for low, high in ((0, split), (split, vocab_local)):
+        logits = contract_last(chosen, lax.all_gather(head_table[low:high], "dp", axis=1, tiled=True))
+        vocab_iota = jnp.arange(low, high, dtype=jnp.int32)
+        target_hits = local_target[:, None] == vocab_iota[None, :]
+        part_maxima = jnp.max(logits, axis=1)
+        shifted = logits - part_maxima[:, None]
+        weights = jnp.exp(shifted)
+        parts.append(
+            jnp.stack(
+                [
+                    part_maxima,
+                    jnp.sum(weights, axis=1),
+                    jnp.sum(weights * shifted, axis=1),
+                    jnp.sum(jnp.where(target_hits, logits, 0.0), axis=1),
+                ],
+                axis=1,
+            )
+        )
+    stats = jnp.stack(parts, axis=1)
+    gathered = lax.all_to_all(stats.reshape(devices, owned_count, 2, 4), TENSOR, 0, 0, tiled=True)
+    gathered = gathered.transpose(0, 2, 1, 3).reshape(devices * 2, owned_count, 4)
     part_max = gathered[:, :, 0]
     maxima = jnp.max(part_max, axis=0)
     gap = part_max - maxima[None, :]

time: 169 us -> 196 us (1.16)
  waiting for transfers between devices: 40.1 us -> 61.9 us
  local copies, waits for them, and re-layouts: 4.58 us -> 11 us
    all_gather x1 -> x2, waiting for transfers between devices: 14.9 us -> 32.5 us  [body(): lax.all_gather(head_table[low:high], 'dp', axis=1, tiled=True)]
    all_to_all x1, waiting for transfers between devices: 14.8 us -> 19.7 us  [body(): lax.all_to_all(stats.reshape(devices, owned_count, 2, 4), TENSOR, 0, 0, t...]
    slice x1 -> x2, local copies, waits for them, and re-layouts: 0.07 us -> 3.44 us  [body(): head_table[low:high]]
    dot_general x1 -> x2, matrix products: 11.9 us -> 12.3 us  [contract_last(): lax.dot_general(left, right, (((1,), (1,)), ((), ())), preferred_element_...]
  transfers between devices with their start and end apart: 3 -> 4, of which waited for: 3 -> 3; matrix products, arithmetic and copies ran while one was open for 3% -> 8% of each run, Pallas kernels for 0% -> 0%
where the time goes in v4:
time: 196 us; the launch traced here: 193 us
  blocking collectives  68.8 us (35%)
  waiting for transfers between devices  61.9 us (32%)
  starting transfers between devices  18.9 us (10%)
  between operations  15 us (8%)
  matrix products  12.7 us (6%)
  local copies, waits for them, and re-layouts  11 us (6%)
  other arithmetic  5.14 us (3%)
    all_gather x2, waiting for transfers between devices, body(): lax.all_gather(head_table[low:high], 'dp', axis=1, tiled=True)  32.5 us
    all_to_all x1, blocking collectives, body(): arrived = lax.all_to_all(near, 'tz', 0, 0, tiled=True)  31 us
    all_to_all x1, blocking collectives, body(): lax.all_to_all(jnp.broadcast_to(owned_normed[None], (devices // ring, own...  22.3 us
    all_to_all x1, waiting for transfers between devices, body(): lax.all_to_all(stats.reshape(devices, owned_count, 2, 4), TENSOR, 0, 0, t...  19.7 us
    all_to_all x1, blocking collectives, body(): near = lax.all_to_all(by_y, 'ty', 0, 0, tiled=True)  15.5 us
    all_to_all x1, starting transfers between devices, body(): lax.all_to_all(stats.reshape(devices, owned_count, 2, 4), TENSOR, 0, 0, t...  15.4 us
    dot_general x2, matrix products, contract_last(): lax.dot_general(left, right, (((1,), (1,)), ((), ())), preferred_element_...  12.3 us
    all_to_all x1, waiting for transfers between devices, body(): lax.all_to_all(jnp.broadcast_to(along_z[None], (ring, devices // ring, ow...  9.67 us
  transfers between devices with their start and end apart: 4, of which 3 were waited for; matrix products, arithmetic and copies ran while one was open for 8% of the time, Pallas kernels for 0%

profile of v4, /device:TPU:1, one launch (start us, length us, event | category | flops | bytes accessed | tf_op | source)
XLA Modules:
  0.0 193.5 jit_solution(13988544709984714789)
XLA Ops:
  7.2 2.4 %slice.19 = bf16[1952,256]{1,0:T(8,128)(2,1)} slice(bf16[3920,256]{1,0:T(8,128)(2,1)} %param.11), slice={[0:1952], [0:256]} | slice | bytes 1998848 | tf_op jit(solution)/shard_map/slice | solution.py:57
  9.7 1.0 slice.20
  10.8 0.5 convolution_convert_fusion
  11.3 0.4 reshape.125
  11.7 0.5 copy.70
  12.2 15.5 %all_to_all.25 = bf16[4,16,4,2048]{3,2,1,0:T(4,128)(2,1)S(1)} all-to-all(bf16[4,16,4,2048]{3,2,1,0:T(4,128)(2,1)S(1)} %bitcast.15), channel_id=1, replica_groups=mesh['dp'=8,'tz'=16,'ty'=4] {'ty'}, dimensions={0} | all-to-all | bytes 2097152 | tf_op jit(solution)/shard_map/all_to_all | solution.py:39
  27.7 0.7 reduce_sum.124
  28.4 31.0 %all_to_all.26 = bf16[16,4,2048]{2,1,0:T(4,128)(2,1)S(1)} all-to-all(bf16[16,4,2048]{2,1,0:T(4,128)(2,1)S(1)} %reduce_sum.124), channel_id=1, replica_groups=mesh['dp'=8,'tz'=16,'ty'=4] {'tz'}, dimensions={0} | all-to-all | bytes 524288 | tf_op jit(solution)/shard_map/all_to_all | solution.py:41
  59.5 0.4 convert_reduce_fusion
  59.9 0.2 multiply_reduce_fusion
  60.3 22.3 %all_to_all.27 = bf16[16,4,2048]{2,1,0:T(4,128)(2,1)S(1)} all-to-all(bf16[16,4,2048]{2,1,0:T(4,128)(2,1)S(1)} %broadcast_in_dim.26), channel_id=1, replica_groups=mesh['dp'=8,'tz'=16,'ty'=4] {'tz'}, dimensions={0} | all-to-all | bytes 524288 | tf_op jit(solution)/shard_map/all_to_all | solution.py:44
  82.6 1.5 broadcast_in_dim.27
  84.1 3.5 %all-to-all-start.3 = ((bf16[4,16,4,2048]{3,2,1,0:T(4,128)(2,1)}), bf16[4,16,4,2048]{3,2,1,0:T(4,128)(2,1)S(1)}, u32[]{:S(2)}, u32[]{:S(2)}) async-start(bf16[4,16,4,2048]{3,2,1,0:T(4,128)(2,1)} %broadcast_in_dim.27), calls=%async_computation.3 | async-start | bytes 2097152 | tf_op jit(solution)/shard_map/all_to_all | solution.py:47
  87.6 9.7 %all-to-all-done.3 = bf16[4,16,4,2048]{3,2,1,0:T(4,128)(2,1)S(1)} async-done(((bf16[4,16,4,2048]{3,2,1,0:T(4,128)(2,1)}), bf16[4,16,4,2048]{3,2,1,0:T(4,128)(2,1)S(1)}, u32[]{:S(2)}, u32[]{:S(2)}) %all-to-all-start.3) | async-done | bytes 1048608 | tf_op jit(solution)/shard_map/all_to_all | solution.py:47
  97.3 0.6 copy.56
  97.9 1.1 reshape.126
  99.0 6.2 %fusion.4 = (f32[256]{0:T(256)S(1)}, f32[256,1952]{0,1:T(8,128)S(1)}) fusion(bf16[256,2048]{1,0:T(8,128)(2,1)} %reshape.126, bf16[1952,2048]{1,0:T(8,128)(2,1)} %all-gather.3.cloned.1.call-done), kind=kOutput, calls=%fused_computation.40 | convolution fusion | flops 2047319808 | bytes 11043840 | tf_op jit(solution)/shard_map/dot_general | solution.py:19
  105.3 0.7 exponential_reduce_fusion.1
  106.2 0.1 stack.37
  106.4 0.1 stack.36
  106.6 32.5 %all-gather.5.cloned.1.call-done = bf16[1968,2048]{1,0:T(8,128)(2,1)} async-done(((bf16[1968,256]{1,0:T(8,128)(2,1)}), bf16[1968,2048]{1,0:T(8,128)(2,1)}) %all-gather.5.cloned.1.call-update) | async-done | bytes 8060944 | tf_op jit(solution)/shard_map/all_gather | solution.py:57
  139.2 6.1 %fusion.3 = (f32[256]{0:T(256)S(1)}, f32[256,1968]{0,1:T(8,128)S(1)}) fusion(bf16[256,2048]{1,0:T(8,128)(2,1)} %reshape.126, bf16[1968,2048]{1,0:T(8,128)(2,1)} %all-gather.5.cloned.1.call-done), kind=kOutput, calls=%fused_computation.39 | convolution fusion | flops 2064101120 | bytes 11125760 | tf_op jit(solution)/shard_map/dot_general | solution.py:19
  145.4 1.0 exponential_reduce_fusion
  146.6 0.1 stack.42
  147.1 0.9 copy.65
  147.9 15.4 %all-to-all-start.4 = ((f32[64,4,2,4]{1,3,2,0:T(4,128)}), f32[64,4,2,4]{1,3,2,0:T(4,128)S(1)}, u32[]{:S(2)}, u32[]{:S(2)}) async-start(f32[64,4,2,4]{1,3,2,0:T(4,128)} %copy.65), calls=%async_computation.4 | async-start | bytes 524288 | tf_op jit(solution)/shard_map/all_to_all | solution.py:75
  164.0 19.7 %all-to-all-done.4 = f32[64,4,2,4]{1,3,2,0:T(4,128)S(1)} async-done(((f32[64,4,2,4]{1,3,2,0:T(4,128)}), f32[64,4,2,4]{1,3,2,0:T(4,128)S(1)}, u32[]{:S(2)}, u32[]{:S(2)}) %all-to-all-start.4) | async-done | bytes 8224 | tf_op jit(solution)/shard_map/all_to_all | solution.py:75
  183.7 1.0 copy.66
  184.7 0.6 slice_reduce_fusion
  185.3 0.2 multiply_reduce_fusion.1
  185.5 0.6 subtract_select_fusion
  186.1 0.5 subtract_select_fusion.1
  (40 shorter events, 1.5 us)
Async XLA Ops:
  7.2 3.7 %copy-start = (bf16[128,2048]{1,0:T(8,128)(2,1)S(1)}, bf16[128,2048]{1,0:T(8,128)(2,1)}, u32[]{:S(2)}) copy-start(bf16[128,2048]{1,0:T(8,128)(2,1)} %param.8) | copy-start | bytes 1572868
  7.2 2.5 %copy-start.1 = (bf16[3920,256]{1,0:T(8,128)(2,1)S(1)}, bf16[3920,256]{1,0:T(8,128)(2,1)}, u32[]{:S(2)}) copy-start(bf16[3920,256]{1,0:T(8,128)(2,1)} %param.11) | copy-start | bytes 6021124
  7.2 91.8 %all-gather.3.cloned.1.call-start = ((), (), s32[]{:S(2)}) async-start(), calls=%async_computation.5 | async-start | bytes 8994816 | tf_op jit(solution)/shard_map/all_gather | solution.py:57
  9.6 1.2 copy-start.4
  9.7 129.5 %all-gather.5.cloned.1.call-start = ((), (), s32[]{:S(2)}) async-start(), calls=%async_computation.6 | async-start | bytes 9068544 | tf_op jit(solution)/shard_map/all_gather | solution.py:57
  12.2 47.9 %copy-start.2 = (f32[2048]{0:T(1024)S(1)}, f32[2048]{0:T(1024)}, u32[]{:S(2)}) copy-start(f32[2048]{0:T(1024)} %param.10) | copy-start | bytes 24580
  12.2 47.9 %copy-start.3 = (f32[2048]{0:T(1024)S(1)}, f32[2048]{0:T(1024)}, u32[]{:S(2)}) copy-start(f32[2048]{0:T(1024)} %param.9) | copy-start | bytes 24580
  60.3 27.3 %copy-start.5 = (s32[256]{0:T(256)S(1)}, s32[256]{0:T(256)}, u32[]{:S(2)}) copy-start(s32[256]{0:T(256)} %param.14) | copy-start | bytes 3076
  84.1 13.2 %all-to-all-start.3 = ((bf16[4,16,4,2048]{3,2,1,0:T(4,128)(2,1)}), bf16[4,16,4,2048]{3,2,1,0:T(4,128)(2,1)S(1)}, u32[]{:S(2)}, u32[]{:S(2)}) async-start(bf16[4,16,4,2048]{3,2,1,0:T(4,128)(2,1)} %broadcast_in_dim.27), calls=%async_computation.3 | async-start | bytes 2097152 | tf_op jit(solution)/shard_map/all_to_all | solution.py:47
  145.3 40.2 %copy-start.6 = (s32[256]{0:T(256)S(1)}, s32[256]{0:T(256)}, u32[]{:S(2)}) copy-start(s32[256]{0:T(256)} %param.15) | copy-start | bytes 3076
  147.9 35.7 %all-to-all-start.4 = ((f32[64,4,2,4]{1,3,2,0:T(4,128)}), f32[64,4,2,4]{1,3,2,0:T(4,128)S(1)}, u32[]{:S(2)}, u32[]{:S(2)}) async-start(f32[64,4,2,4]{1,3,2,0:T(4,128)} %copy.65), calls=%async_computation.4 | async-start | bytes 524288 | tf_op jit(solution)/shard_map/all_to_all | solution.py:75
Sparse Core Ops, SparseCore 0:
  10.1 65.6 all-gather.2
  78.0 61.1 all-gather.4

commit v5 on v3

--- a/solution.py
+++ b/solution.py
@@ -49,7 +49,13 @@
     )
     chosen = along_y.transpose(1, 0, 2, 3).reshape(scored_count, width)
 
-    logits = contract_last(chosen, lax.all_gather(head_table, "dp", axis=1, tiled=True))
+    blocks = lax.all_gather(head_table, "dp", axis=0, tiled=False)
+    logits = lax.dot_general(
+        chosen.reshape(scored_count, blocks.shape[0], blocks.shape[2]),
+        blocks,
+        (((1, 2), (0, 2)), ((), ())),
+        preferred_element_type=jnp.float32,
+    )
     vocab_local = head_table.shape[0]
     vocab_iota = jnp.arange(vocab_local, dtype=jnp.int32)
     target_hits = (targets - position * vocab_local)[:, None] == vocab_iota[None, :]

time: 169 us -> 163 us (0.964)
  waiting for transfers between devices: 40.1 us -> 34.3 us
    all_gather x1, waiting for transfers between devices: 14.9 us -> 9.07 us  [body(): blocks = lax.all_gather(head_table, 'dp', axis=0, tiled=False)]
  transfers between devices with their start and end apart: 3 -> 3, of which waited for: 3 -> 3; matrix products, arithmetic and copies ran while one was open for 3% -> 4% of each run, Pallas kernels for 0% -> 0%
where the time goes in v5:
time: 163 us; the launch traced here: 161 us
  blocking collectives  68.8 us (42%)
  waiting for transfers between devices  34.3 us (21%)
  starting transfers between devices  18.9 us (12%)
  between operations  14.9 us (9%)
  matrix products  12.3 us (8%)
  other arithmetic  7.06 us (4%)
  local copies, waits for them, and re-layouts  5.06 us (3%)
    all_to_all x1, blocking collectives, body(): arrived = lax.all_to_all(near, 'tz', 0, 0, tiled=True)  31 us
    all_to_all x1, blocking collectives, body(): lax.all_to_all(jnp.broadcast_to(owned_normed[None], (devices // ring, own...  22.3 us
    all_to_all x1, blocking collectives, body(): near = lax.all_to_all(by_y, 'ty', 0, 0, tiled=True)  15.5 us
    all_to_all x1, starting transfers between devices, body(): lax.all_to_all(stats.reshape(devices, owned_count, 4), TENSOR, 0, 0, tile...  15.4 us
    all_to_all x1, waiting for transfers between devices, body(): lax.all_to_all(stats.reshape(devices, owned_count, 4), TENSOR, 0, 0, tile...  14.8 us
    dot_general x1, matrix products, body(): lax.dot_general(chosen.reshape(scored_count, blocks.shape[0], blocks.shap...  11.8 us
    all_to_all x1, waiting for transfers between devices, body(): lax.all_to_all(jnp.broadcast_to(along_z[None], (ring, devices // ring, ow...  9.73 us
    all_gather x1, waiting for transfers between devices, body(): blocks = lax.all_gather(head_table, 'dp', axis=0, tiled=False)  9.07 us
  transfers between devices with their start and end apart: 3, of which 3 were waited for; matrix products, arithmetic and copies ran while one was open for 4% of the time, Pallas kernels for 0%

profile of v5, /device:TPU:1, one launch (start us, length us, event | category | flops | bytes accessed | tf_op | source)
XLA Modules:
  0.0 161.4 jit_solution(15681048161779239786)
XLA Ops:
  7.2 0.7 all-gather.3.cloned.1.call-update
  7.9 0.7 broadcast_subtract_fusion.1
  8.6 0.5 convolution_convert_fusion
  9.1 0.4 reshape.102
  9.5 0.5 copy.60
  10.0 15.5 %all_to_all.25 = bf16[4,16,4,2048]{3,2,1,0:T(4,128)(2,1)S(1)} all-to-all(bf16[4,16,4,2048]{3,2,1,0:T(4,128)(2,1)S(1)} %bitcast.35), channel_id=1, replica_groups=mesh['dp'=8,'tz'=16,'ty'=4] {'ty'}, dimensions={0} | all-to-all | bytes 2097152 | tf_op jit(solution)/shard_map/all_to_all | solution.py:39
  25.5 0.7 reduce_sum.97
  26.3 31.0 %all_to_all.26 = bf16[16,4,2048]{2,1,0:T(4,128)(2,1)S(1)} all-to-all(bf16[16,4,2048]{2,1,0:T(4,128)(2,1)S(1)} %reduce_sum.97), channel_id=1, replica_groups=mesh['dp'=8,'tz'=16,'ty'=4] {'tz'}, dimensions={0} | all-to-all | bytes 524288 | tf_op jit(solution)/shard_map/all_to_all | solution.py:41
  57.3 0.4 convert_reduce_fusion
  57.7 0.2 multiply_reduce_fusion
  57.9 0.1 add_convert_fusion
  58.0 0.1 broadcast_in_dim.22
  58.1 22.3 %all_to_all.27 = bf16[16,4,2048]{2,1,0:T(4,128)(2,1)S(1)} all-to-all(bf16[16,4,2048]{2,1,0:T(4,128)(2,1)S(1)} %broadcast_in_dim.22), channel_id=1, replica_groups=mesh['dp'=8,'tz'=16,'ty'=4] {'tz'}, dimensions={0} | all-to-all | bytes 524288 | tf_op jit(solution)/shard_map/all_to_all | solution.py:44
  80.4 1.5 broadcast_in_dim.23
  81.9 3.5 %all-to-all-start.3 = ((bf16[4,16,4,2048]{3,2,1,0:T(4,128)(2,1)}), bf16[4,16,4,2048]{3,2,1,0:T(4,128)(2,1)S(1)}, u32[]{:S(2)}, u32[]{:S(2)}) async-start(bf16[4,16,4,2048]{3,2,1,0:T(4,128)(2,1)} %broadcast_in_dim.23), calls=%async_computation.3 | async-start | bytes 2097152 | tf_op jit(solution)/shard_map/all_to_all | solution.py:47
  85.4 9.7 %all-to-all-done.3 = bf16[4,16,4,2048]{3,2,1,0:T(4,128)(2,1)S(1)} async-done(((bf16[4,16,4,2048]{3,2,1,0:T(4,128)(2,1)}), bf16[4,16,4,2048]{3,2,1,0:T(4,128)(2,1)S(1)}, u32[]{:S(2)}, u32[]{:S(2)}) %all-to-all-start.3) | async-done | bytes 1048608 | tf_op jit(solution)/shard_map/all_to_all | solution.py:47
  95.2 0.5 copy.44
  95.6 0.8 reshape_reshape.3
  96.4 9.1 %all-gather.3.cloned.1.call-done = bf16[31360,256]{1,0:T(8,128)(2,1)} async-done(((bf16[3920,256]{1,0:T(8,128)(2,1)}), bf16[31360,256]{1,0:T(8,128)(2,1)}) %all-gather.3.cloned.1.call-update) | async-done | bytes 16056336 | tf_op jit(solution)/shard_map/all_gather | solution.py:52
  105.5 11.8 %fusion.7 = (f32[256]{0:T(256)S(1)}, f32[256,3920]{0,1:T(8,128)}) fusion(bf16[8,3920,256]{2,1,0:T(8,128)(2,1)} %bitcast.36, bf16[256,8,256]{2,1,0:T(8,128)(2,1)S(1)} %reshape_reshape.3), kind=kOutput, calls=%fused_computation.39 | convolution fusion | flops 4111421184 | bytes 21120000 | tf_op jit(solution)/shard_map/dot_general | solution.py:53
  117.3 0.1 stack.15
  117.4 3.4 %exponential_reduce_fusion = (f32[256]{0:T(256)S(1)}, f32[256]{0:T(256)S(1)}, f32[256]{0:T(256)S(1)}) fusion(f32[256,3920]{0,1:T(8,128)} %get-tuple-element.17, f32[256]{0:T(256)S(1)} %get-tuple-element.16, s32[256]{0:T(256)S(1)} %broadcast_subtract_fusion), kind=kLoop, calls=%fused_computation.1 | loop fusion | flops 7023872 | bytes 4019200 | tf_op jit(solution)/shard_map/reduce_sum | solution.py:67
  120.9 0.1 stack.16
  121.0 0.1 stack.17
  121.1 0.1 stack.18
  121.2 0.7 copy.46
  122.0 15.4 %all-to-all-start.4 = ((f32[64,4,4]{1,2,0:T(4,128)}), f32[64,4,4]{1,2,0:T(4,128)S(1)}, u32[]{:S(2)}, u32[]{:S(2)}) async-start(f32[64,4,4]{1,2,0:T(4,128)} %copy.46), calls=%async_computation.4 | async-start | bytes 262144 | tf_op jit(solution)/shard_map/all_to_all | solution.py:69
  138.0 14.8 %all-to-all-done.4 = f32[64,4,4]{1,2,0:T(4,128)S(1)} async-done(((f32[64,4,4]{1,2,0:T(4,128)}), f32[64,4,4]{1,2,0:T(4,128)S(1)}, u32[]{:S(2)}, u32[]{:S(2)}) %all-to-all-start.4) | async-done | bytes 4128 | tf_op jit(solution)/shard_map/all_to_all | solution.py:69
  152.8 0.1 slice_reduce_fusion.1
  153.2 0.2 fusion.4
  153.4 0.6 subtract_select_fusion
  154.0 0.5 subtract_select_fusion.1
  (20 shorter events, 0.3 us)
Async XLA Ops:
  7.2 1.4 copy-start
  7.2 98.3 %all-gather.3.cloned.1.call-start = ((), (), s32[]{:S(2)}) async-start(), calls=%async_computation.5 | async-start | bytes 18063360 | tf_op jit(solution)/shard_map/all_gather | solution.py:52
  9.1 48.8 %copy-start.1 = (f32[2048]{0:T(1024)S(1)}, f32[2048]{0:T(1024)}, u32[]{:S(2)}) copy-start(f32[2048]{0:T(1024)} %param.10) | copy-start | bytes 24580
  9.1 48.8 %copy-start.2 = (f32[2048]{0:T(1024)S(1)}, f32[2048]{0:T(1024)}, u32[]{:S(2)}) copy-start(f32[2048]{0:T(1024)} %param.9) | copy-start | bytes 24580
  10.0 75.4 %copy-start.4 = (s32[256]{0:T(256)S(1)}, s32[256]{0:T(256)}, u32[]{:S(2)}) copy-start(s32[256]{0:T(256)} %param.14) | copy-start | bytes 3076
  81.9 13.3 %all-to-all-start.3 = ((bf16[4,16,4,2048]{3,2,1,0:T(4,128)(2,1)}), bf16[4,16,4,2048]{3,2,1,0:T(4,128)(2,1)S(1)}, u32[]{:S(2)}, u32[]{:S(2)}) async-start(bf16[4,16,4,2048]{3,2,1,0:T(4,128)(2,1)} %broadcast_in_dim.23), calls=%async_computation.3 | async-start | bytes 2097152 | tf_op jit(solution)/shard_map/all_to_all | solution.py:47
  117.3 36.0 %copy-start.3 = (s32[256]{0:T(256)S(1)}, s32[256]{0:T(256)}, u32[]{:S(2)}) copy-start(s32[256]{0:T(256)} %param.13) | copy-start | bytes 3076
  117.3 36.1 %copy-start.5 = (s32[256]{0:T(256)S(1)}, s32[256]{0:T(256)}, u32[]{:S(2)}) copy-start(s32[256]{0:T(256)} %param.15) | copy-start | bytes 3076
  122.0 30.9 %all-to-all-start.4 = ((f32[64,4,4]{1,2,0:T(4,128)}), f32[64,4,4]{1,2,0:T(4,128)S(1)}, u32[]{:S(2)}, u32[]{:S(2)}) async-start(f32[64,4,4]{1,2,0:T(4,128)} %copy.46), calls=%async_computation.4 | async-start | bytes 262144 | tf_op jit(solution)/shard_map/all_to_all | solution.py:69
Sparse Core Ops, SparseCore 0:
  10.1 95.2 all-gather.2

commit v6 on v3

--- a/solution.py
+++ b/solution.py
@@ -2,9 +2,12 @@
 import jax.numpy as jnp
 from jax import lax
 from jax.sharding import Mesh, PartitionSpec as P
+from jax.experimental import pallas as pl
+from jax.experimental.pallas import tpu as pltpu
 
 EPSILON = 1e-05
 TENSOR = ("tz", "ty")
+INTERPRET = False
 
 
 def layer_norm(states, norm_gain, norm_bias):
@@ -19,6 +22,74 @@
     return lax.dot_general(
         left, right, (((1,), (1,)), ((), ())), preferred_element_type=jnp.float32
     )
+
+
+def tile_of(vocab):
+    best = vocab
+    for size in range(8, 641, 8):
+        if vocab % size == 0:
+            best = size
+    return best
+
+
+def head_stats_kernel(chosen_ref, blocks_ref, target_ref, out_ref):
+    step = pl.program_id(0)
+    count, tile, part = blocks_ref.shape
+    logits = jnp.zeros((tile, chosen_ref.shape[0]), jnp.float32)
+    for block in range(count):
+        logits = logits + lax.dot_general(
+            blocks_ref[block],
+            chosen_ref[:, block * part:(block + 1) * part],
+            (((1,), (1,)), ((), ())),
+            preferred_element_type=jnp.float32,
+        )
+    tile_max = jnp.max(logits, axis=0, keepdims=True)
+    vocab_iota = lax.broadcasted_iota(jnp.int32, logits.shape, 0) + step * tile
+    hit = jnp.sum(jnp.where(vocab_iota == target_ref[...], logits, 0.0), axis=0, keepdims=True)
+
+    @pl.when(step == 0)
+    def _():
+        shifted = logits - tile_max
+        weights = jnp.exp(shifted)
+        out_ref[0:1, :] = tile_max
+        out_ref[1:2, :] = jnp.sum(weights, axis=0, keepdims=True)
+        out_ref[2:3, :] = jnp.sum(weights * shifted, axis=0, keepdims=True)
+        out_ref[3:4, :] = hit
+
+    @pl.when(step > 0)
+    def _():
+        old_max = out_ref[0:1, :]
+        old_total = out_ref[1:2, :]
+        new_max = jnp.maximum(old_max, tile_max)
+        shifted = logits - new_max
+        weights = jnp.exp(shifted)
+        gap = old_max - new_max
+        scale = jnp.exp(gap)
+        out_ref[0:1, :] = new_max
+        out_ref[1:2, :] = scale * old_total + jnp.sum(weights, axis=0, keepdims=True)
+        out_ref[2:3, :] = scale * (out_ref[2:3, :] + gap * old_total) + jnp.sum(
+            weights * shifted, axis=0, keepdims=True
+        )
+        out_ref[3:4, :] = out_ref[3:4, :] + hit
+
+
+def head_stats(chosen, blocks, local_target):
+    count, vocab, part = blocks.shape
+    slots, width = chosen.shape
+    tile = tile_of(vocab)
+    return pl.pallas_call(
+        head_stats_kernel,
+        grid=(vocab // tile,),
+        in_specs=[
+            pl.BlockSpec((slots, width), lambda step: (0, 0)),
+            pl.BlockSpec((count, tile, part), lambda step: (0, step, 0)),
+            pl.BlockSpec((1, slots), lambda step: (0, 0)),
+        ],
+        out_specs=pl.BlockSpec((8, slots), lambda step: (0, 0)),
+        out_shape=jax.ShapeDtypeStruct((8, slots), jnp.float32),
+        compiler_params=pltpu.CompilerParams(dimension_semantics=("arbitrary",)),
+        interpret=INTERPRET,
+    )(chosen, blocks, local_target.reshape(1, slots))
 
 
 def body(states, norm_gain, norm_bias, head_table, seq_lengths, scored_index, targets, slot_mask):
@@ -49,17 +120,9 @@
     )
     chosen = along_y.transpose(1, 0, 2, 3).reshape(scored_count, width)
 
-    logits = contract_last(chosen, lax.all_gather(head_table, "dp", axis=1, tiled=True))
+    blocks = lax.all_gather(head_table, "dp", axis=0, tiled=False)
     vocab_local = head_table.shape[0]
-    vocab_iota = jnp.arange(vocab_local, dtype=jnp.int32)
-    target_hits = (targets - position * vocab_local)[:, None] == vocab_iota[None, :]
-    target_part = jnp.sum(jnp.where(target_hits, logits, 0.0), axis=1)
-    local_maxima = jnp.max(logits, axis=1)
-    shifted = logits - local_maxima[:, None]
-    weights = jnp.exp(shifted)
-    stats = jnp.stack(
-        [local_maxima, jnp.sum(weights, axis=1), jnp.sum(weights * shifted, axis=1), target_part], axis=1
-    )
+    stats = head_stats(chosen, blocks, targets - position * vocab_local)[:4].T
     gathered = lax.all_to_all(stats.reshape(devices, owned_count, 4), TENSOR, 0, 0, tiled=True)
     part_max = gathered[:, :, 0]
     maxima = jnp.max(part_max, axis=0)

time: 169 us -> 159 us (0.941)
  matrix products: 12.3 us -> 0.47 us
  Pallas kernels: 0 us -> 11.5 us
  waiting for transfers between devices: 40.1 us -> 33.3 us
  other arithmetic: 7.06 us -> 3.96 us
    dot_general x1 -> x0, matrix products: 11.9 us -> none  [contract_last(): lax.dot_general(left, right, (((1,), (1,)), ((), ())), preferred_element_...]
    pallas_call x0 -> x1, Pallas kernels: none -> 11.5 us  [head_stats(): pl.pallas_call(head_stats_kernel, grid=(vocab // tile,), in_specs=[pl.Blo...]
    all_gather x1, waiting for transfers between devices: 14.9 us -> 8.65 us  [body(): blocks = lax.all_gather(head_table, 'dp', axis=0, tiled=False)]
    reduce_sum x1, other arithmetic: 3.45 us -> 0.12 us  [body(): target_logit = jnp.sum(gathered[:, :, 3], axis=0)]
  transfers between devices with their start and end apart: 3 -> 3, of which waited for: 3 -> 3; matrix products, arithmetic and copies ran while one was open for 3% -> 5% of each run, Pallas kernels for 0% -> 0%
where the time goes in v6:
time: 159 us; the launch traced here: 158 us
  blocking collectives  68.8 us (43%)
  waiting for transfers between devices  33.3 us (21%)
  starting transfers between devices  18.9 us (12%)
  between operations  14.8 us (9%)
  Pallas kernels  11.5 us (7%)
  local copies, waits for them, and re-layouts  5.77 us (4%)
  other arithmetic  3.96 us (2%)
    all_to_all x1, blocking collectives, body(): arrived = lax.all_to_all(near, 'tz', 0, 0, tiled=True)  31 us
    all_to_all x1, blocking collectives, body(): lax.all_to_all(jnp.broadcast_to(owned_normed[None], (devices // ring, own...  22.3 us
    all_to_all x1, blocking collectives, body(): near = lax.all_to_all(by_y, 'ty', 0, 0, tiled=True)  15.5 us
    all_to_all x1, starting transfers between devices, body(): lax.all_to_all(stats.reshape(devices, owned_count, 4), TENSOR, 0, 0, tile...  15.4 us
    all_to_all x1, waiting for transfers between devices, body(): lax.all_to_all(stats.reshape(devices, owned_count, 4), TENSOR, 0, 0, tile...  14.8 us
    pallas_call x1, Pallas kernels, head_stats(): pl.pallas_call(head_stats_kernel, grid=(vocab // tile,), in_specs=[pl.Blo...  11.5 us
    all_to_all x1, waiting for transfers between devices, body(): lax.all_to_all(jnp.broadcast_to(along_z[None], (ring, devices // ring, ow...  9.15 us
    all_gather x1, waiting for transfers between devices, body(): blocks = lax.all_gather(head_table, 'dp', axis=0, tiled=False)  8.65 us
  transfers between devices with their start and end apart: 3, of which 3 were waited for; matrix products, arithmetic and copies ran while one was open for 5% of the time, Pallas kernels for 0%

profile of v6, /device:TPU:1, one launch (start us, length us, event | category | flops | bytes accessed | tf_op | source)
XLA Modules:
  0.0 157.6 jit_solution(15952586649449358001)
XLA Ops:
  7.2 0.0 copy-start
  7.2 0.0 all-gather.3.cloned.1.call-start
  7.2 0.7 all-gather.3.cloned.1.call-update
  7.9 0.7 broadcast_subtract_fusion.1
  8.6 0.5 convolution_convert_fusion
  9.1 0.4 reshape.100
  9.5 0.5 copy.38
  10.0 0.0 copy-start.2
  10.0 15.5 %all_to_all.25 = bf16[4,16,4,2048]{3,2,1,0:T(4,128)(2,1)S(1)} all-to-all(bf16[4,16,4,2048]{3,2,1,0:T(4,128)(2,1)S(1)} %bitcast.22), channel_id=1, replica_groups=mesh['dp'=8,'tz'=16,'ty'=4] {'ty'}, dimensions={0} | all-to-all | bytes 2097152 | tf_op jit(solution)/shard_map/all_to_all | solution.py:110
  25.5 0.7 reduce_sum.70
  26.2 31.0 %all_to_all.26 = bf16[16,4,2048]{2,1,0:T(4,128)(2,1)S(1)} all-to-all(bf16[16,4,2048]{2,1,0:T(4,128)(2,1)S(1)} %reduce_sum.70), channel_id=1, replica_groups=mesh['dp'=8,'tz'=16,'ty'=4] {'tz'}, dimensions={0} | all-to-all | bytes 524288 | tf_op jit(solution)/shard_map/all_to_all | solution.py:112
  57.2 0.4 convert_reduce_fusion
  57.6 0.2 multiply_reduce_fusion.2
  57.8 0.1 add_convert_fusion
  57.9 0.1 broadcast_in_dim.18
  58.0 22.3 %all_to_all.27 = bf16[16,4,2048]{2,1,0:T(4,128)(2,1)S(1)} all-to-all(bf16[16,4,2048]{2,1,0:T(4,128)(2,1)S(1)} %broadcast_in_dim.18), channel_id=1, replica_groups=mesh['dp'=8,'tz'=16,'ty'=4] {'tz'}, dimensions={0} | all-to-all | bytes 524288 | tf_op jit(solution)/shard_map/all_to_all | solution.py:115
  80.3 1.5 broadcast_in_dim.19
  81.8 3.5 %all-to-all-start.3 = ((bf16[4,16,4,2048]{3,2,1,0:T(4,128)(2,1)}), bf16[4,16,4,2048]{3,2,1,0:T(4,128)(2,1)S(1)}, u32[]{:S(2)}, u32[]{:S(2)}) async-start(bf16[4,16,4,2048]{3,2,1,0:T(4,128)(2,1)} %broadcast_in_dim.19), calls=%async_computation.3 | async-start | bytes 2097152 | tf_op jit(solution)/shard_map/all_to_all | solution.py:118
  85.4 0.6 broadcast_subtract_fusion
  86.0 9.1 %all-to-all-done.3 = bf16[4,16,4,2048]{3,2,1,0:T(4,128)(2,1)S(1)} async-done(((bf16[4,16,4,2048]{3,2,1,0:T(4,128)(2,1)}), bf16[4,16,4,2048]{3,2,1,0:T(4,128)(2,1)S(1)}, u32[]{:S(2)}, u32[]{:S(2)}) %all-to-all-start.3) | async-done | bytes 1048608 | tf_op jit(solution)/shard_map/all_to_all | solution.py:118
  95.1 0.6 copy.29
  95.7 1.1 reshape.101.chosen_ref
  96.8 8.6 %all-gather.3.cloned.1.call-done = bf16[31360,256]{1,0:T(8,128)(2,1)} async-done(((bf16[3920,256]{1,0:T(8,128)(2,1)}), bf16[31360,256]{1,0:T(8,128)(2,1)}) %all-gather.3.cloned.1.call-update) | async-done | bytes 16056336 | tf_op jit(solution)/shard_map/all_gather | solution.py:123
  105.5 11.5 %shard_map.95 = f32[8,256]{1,0:T(8,128)} custom-call(bf16[256,2048]{1,0:T(8,128)(2,1)} %reshape.101.chosen_ref, bf16[8,3920,256]{2,1,0:T(8,128)(2,1)} %bitcast.20, s32[1,256]{1,0:T(1,128)} %bitcast.27), custom_call_target="tpu_custom_call" | custom-call | tf_op jit(solution)/shard_map/pallas_call | solution.py:80
  117.0 0.7 slice_bitcast_fusion
  117.7 0.1 reshape.103
  117.9 0.7 copy.30
  118.6 15.4 %all-to-all-start.4 = ((f32[64,4,4]{1,2,0:T(4,128)}), f32[64,4,4]{1,2,0:T(4,128)S(1)}, u32[]{:S(2)}, u32[]{:S(2)}) async-start(f32[64,4,4]{1,2,0:T(4,128)} %copy.30), calls=%async_computation.4 | async-start | bytes 262144 | tf_op jit(solution)/shard_map/all_to_all | solution.py:126
  134.6 14.8 %all-to-all-done.4 = f32[64,4,4]{1,2,0:T(4,128)S(1)} async-done(((f32[64,4,4]{1,2,0:T(4,128)}), f32[64,4,4]{1,2,0:T(4,128)S(1)}, u32[]{:S(2)}, u32[]{:S(2)}) %all-to-all-start.4) | async-done | bytes 4128 | tf_op jit(solution)/shard_map/all_to_all | solution.py:126
  149.5 0.1 slice_reduce_fusion
  149.7 0.6 subtract_select_fusion
  150.3 0.5 subtract_select_fusion.1
  (14 shorter events, 0.1 us)
Async XLA Ops:
  7.2 1.4 copy-start
  7.2 98.3 %all-gather.3.cloned.1.call-start = ((), (), s32[]{:S(2)}) async-start(), calls=%async_computation.5 | async-start | bytes 18063360 | tf_op jit(solution)/shard_map/all_gather | solution.py:123
  10.0 47.8 %copy-start.1 = (f32[2048]{0:T(1024)S(1)}, f32[2048]{0:T(1024)}, u32[]{:S(2)}) copy-start(f32[2048]{0:T(1024)} %param.10) | copy-start | bytes 24580
  10.0 47.8 %copy-start.2 = (f32[2048]{0:T(1024)S(1)}, f32[2048]{0:T(1024)}, u32[]{:S(2)}) copy-start(f32[2048]{0:T(1024)} %param.9) | copy-start | bytes 24580
  57.9 27.5 %copy-start.4 = (s32[256]{0:T(256)S(1)}, s32[256]{0:T(256)}, u32[]{:S(2)}) copy-start(s32[256]{0:T(256)} %param.14) | copy-start | bytes 3076
  81.8 13.3 %all-to-all-start.3 = ((bf16[4,16,4,2048]{3,2,1,0:T(4,128)(2,1)}), bf16[4,16,4,2048]{3,2,1,0:T(4,128)(2,1)S(1)}, u32[]{:S(2)}, u32[]{:S(2)}) async-start(bf16[4,16,4,2048]{3,2,1,0:T(4,128)(2,1)} %broadcast_in_dim.19), calls=%async_computation.3 | async-start | bytes 2097152 | tf_op jit(solution)/shard_map/all_to_all | solution.py:118
  105.5 44.2 %copy-start.3 = (s32[256]{0:T(256)S(1)}, s32[256]{0:T(256)}, u32[]{:S(2)}) copy-start(s32[256]{0:T(256)} %param.13) | copy-start | bytes 3076
  105.5 44.2 %copy-start.5 = (s32[256]{0:T(256)S(1)}, s32[256]{0:T(256)}, u32[]{:S(2)}) copy-start(s32[256]{0:T(256)} %param.15) | copy-start | bytes 3076
  118.6 30.9 %all-to-all-start.4 = ((f32[64,4,4]{1,2,0:T(4,128)}), f32[64,4,4]{1,2,0:T(4,128)S(1)}, u32[]{:S(2)}, u32[]{:S(2)}) async-start(f32[64,4,4]{1,2,0:T(4,128)} %copy.30), calls=%async_computation.4 | async-start | bytes 262144 | tf_op jit(solution)/shard_map/all_to_all | solution.py:126
Sparse Core Ops, SparseCore 0:
  10.1 95.2 all-gather.2

commit v7 on v6

--- a/solution.py
+++ b/solution.py
@@ -118,11 +118,14 @@
     along_y = lax.all_to_all(
         jnp.broadcast_to(along_z[None], (ring, devices // ring, owned_count, width)), "ty", 0, 0, tiled=True
     )
-    chosen = along_y.transpose(1, 0, 2, 3).reshape(scored_count, width)
+    chosen = along_y.reshape(scored_count, width)
 
     blocks = lax.all_gather(head_table, "dp", axis=0, tiled=False)
     vocab_local = head_table.shape[0]
-    stats = head_stats(chosen, blocks, targets - position * vocab_local)[:4].T
+    rings = devices // ring
+    local_target = (targets - position * vocab_local).reshape(rings, ring, owned_count).transpose(1, 0, 2)
+    stats = head_stats(chosen, blocks, local_target.reshape(scored_count))[:4]
+    stats = stats.reshape(4, ring, rings, owned_count).transpose(2, 1, 3, 0)
     gathered = lax.all_to_all(stats.reshape(devices, owned_count, 4), TENSOR, 0, 0, tiled=True)
     part_max = gathered[:, :, 0]
     maxima = jnp.max(part_max, axis=0)

time: 159 us -> 161 us (1.013)
  transfers between devices with their start and end apart: 3 -> 3, of which waited for: 3 -> 3; matrix products, arithmetic and copies ran while one was open for 5% -> 4% of each run, Pallas kernels for 0% -> 0%
where the time goes in v7:
time: 161 us; the launch traced here: 159 us
  blocking collectives  68.8 us (43%)
  waiting for transfers between devices  33.7 us (21%)
  starting transfers between devices  18.9 us (12%)
  between operations  14.9 us (9%)
  Pallas kernels  11.5 us (7%)
  local copies, waits for them, and re-layouts  6.7 us (4%)
  other arithmetic  3.85 us (2%)
    all_to_all x1, blocking collectives, body(): arrived = lax.all_to_all(near, 'tz', 0, 0, tiled=True)  31 us
    all_to_all x1, blocking collectives, body(): lax.all_to_all(jnp.broadcast_to(owned_normed[None], (devices // ring, own...  22.3 us
    all_to_all x1, blocking collectives, body(): near = lax.all_to_all(by_y, 'ty', 0, 0, tiled=True)  15.5 us
    all_to_all x1, starting transfers between devices, body(): lax.all_to_all(stats.reshape(devices, owned_count, 4), TENSOR, 0, 0, tile...  15.4 us
    all_to_all x1, waiting for transfers between devices, body(): lax.all_to_all(stats.reshape(devices, owned_count, 4), TENSOR, 0, 0, tile...  14.8 us
    pallas_call x1, Pallas kernels, head_stats(): pl.pallas_call(head_stats_kernel, grid=(vocab // tile,), in_specs=[pl.Blo...  11.5 us
    all_gather x1, waiting for transfers between devices, body(): blocks = lax.all_gather(head_table, 'dp', axis=0, tiled=False)  9.25 us
    all_to_all x1, waiting for transfers between devices, body(): lax.all_to_all(jnp.broadcast_to(along_z[None], (ring, devices // ring, ow...  8.9 us
  transfers between devices with their start and end apart: 3, of which 3 were waited for; matrix products, arithmetic and copies ran while one was open for 4% of the time, Pallas kernels for 0%

profile of v7, /device:TPU:1, one launch (start us, length us, event | category | flops | bytes accessed | tf_op | source)
XLA Modules:
  0.0 158.8 jit_solution(11479071982011299557)
XLA Ops:
  7.2 0.7 all-gather.3.cloned.1.call-update
  7.9 0.7 broadcast_subtract_fusion.1
  8.6 0.5 convolution_convert_fusion
  9.1 0.4 reshape.103
  9.5 0.5 copy.54
  10.0 15.5 %all_to_all.25 = bf16[4,16,4,2048]{3,2,1,0:T(4,128)(2,1)S(1)} all-to-all(bf16[4,16,4,2048]{3,2,1,0:T(4,128)(2,1)S(1)} %bitcast.34), channel_id=1, replica_groups=mesh['dp'=8,'tz'=16,'ty'=4] {'ty'}, dimensions={0} | all-to-all | bytes 2097152 | tf_op jit(solution)/shard_map/all_to_all | solution.py:110
  25.5 0.7 reduce_sum.70
  26.2 31.0 %all_to_all.26 = bf16[16,4,2048]{2,1,0:T(4,128)(2,1)S(1)} all-to-all(bf16[16,4,2048]{2,1,0:T(4,128)(2,1)S(1)} %reduce_sum.70), channel_id=1, replica_groups=mesh['dp'=8,'tz'=16,'ty'=4] {'tz'}, dimensions={0} | all-to-all | bytes 524288 | tf_op jit(solution)/shard_map/all_to_all | solution.py:112
  57.2 0.4 convert_reduce_fusion
  57.6 0.2 multiply_reduce_fusion
  57.9 0.1 broadcast_in_dim.18
  58.0 22.3 %all_to_all.27 = bf16[16,4,2048]{2,1,0:T(4,128)(2,1)S(1)} all-to-all(bf16[16,4,2048]{2,1,0:T(4,128)(2,1)S(1)} %broadcast_in_dim.18), channel_id=1, replica_groups=mesh['dp'=8,'tz'=16,'ty'=4] {'tz'}, dimensions={0} | all-to-all | bytes 524288 | tf_op jit(solution)/shard_map/all_to_all | solution.py:115
  80.3 1.5 broadcast_in_dim.19
  81.8 3.5 %all-to-all-start.3 = ((bf16[4,16,4,2048]{3,2,1,0:T(4,128)(2,1)}), bf16[4,16,4,2048]{3,2,1,0:T(4,128)(2,1)S(1)}, u32[]{:S(2)}, u32[]{:S(2)}) async-start(bf16[4,16,4,2048]{3,2,1,0:T(4,128)(2,1)} %broadcast_in_dim.19), calls=%async_computation.3 | async-start | bytes 2097152 | tf_op jit(solution)/shard_map/all_to_all | solution.py:118
  85.4 0.1 reshape.105
  85.5 0.7 reshape_reshape.3.target_ref
  86.2 8.9 %all-to-all-done.3 = bf16[4,16,4,2048]{3,2,1,0:T(4,128)(2,1)S(1)} async-done(((bf16[4,16,4,2048]{3,2,1,0:T(4,128)(2,1)}), bf16[4,16,4,2048]{3,2,1,0:T(4,128)(2,1)S(1)}, u32[]{:S(2)}, u32[]{:S(2)}) %all-to-all-start.3) | async-done | bytes 1048608 | tf_op jit(solution)/shard_map/all_to_all | solution.py:118
  95.1 1.1 reshape.104.chosen_ref
  96.2 9.3 %all-gather.3.cloned.1.call-done = bf16[31360,256]{1,0:T(8,128)(2,1)} async-done(((bf16[3920,256]{1,0:T(8,128)(2,1)}), bf16[31360,256]{1,0:T(8,128)(2,1)}) %all-gather.3.cloned.1.call-update) | async-done | bytes 16056336 | tf_op jit(solution)/shard_map/all_gather | solution.py:123
  105.5 11.5 %shard_map.95 = f32[8,256]{1,0:T(8,128)} custom-call(bf16[256,2048]{1,0:T(8,128)(2,1)} %reshape.104.chosen_ref, bf16[8,3920,256]{2,1,0:T(8,128)(2,1)} %bitcast.33, s32[1,256]{1,0:T(1,128)} %reshape_reshape.3.target_ref), custom_call_target="tpu_custom_call" | custom-call | tf_op jit(solution)/shard_map/pallas_call | solution.py:80
  117.0 0.7 slice.21
  117.7 0.1 reshape.106
  117.9 1.1 copy.46
  119.0 15.4 %all-to-all-start.4 = ((f32[64,4,4]{2,1,0:T(4,128)}), f32[64,4,4]{2,1,0:T(4,128)S(1)}, u32[]{:S(2)}, u32[]{:S(2)}) async-start(f32[64,4,4]{2,1,0:T(4,128)} %bitcast.5), calls=%async_computation.4 | async-start | bytes 262144 | tf_op jit(solution)/shard_map/all_to_all | solution.py:129
  135.0 14.8 %all-to-all-done.4 = f32[64,4,4]{2,1,0:T(4,128)S(1)} async-done(((f32[64,4,4]{2,1,0:T(4,128)}), f32[64,4,4]{2,1,0:T(4,128)S(1)}, u32[]{:S(2)}, u32[]{:S(2)}) %all-to-all-start.4) | async-done | bytes 4128 | tf_op jit(solution)/shard_map/all_to_all | solution.py:129
  149.9 0.5 slice_reduce_fusion.1
  150.3 0.1 copy.45
  150.4 0.1 copy.48
  150.5 0.1 copy.49
  150.6 0.2 fusion.2
  150.9 0.6 subtract_select_fusion
  151.5 0.5 subtract_select_fusion.1
  (18 shorter events, 0.2 us)
Async XLA Ops:
  7.2 1.4 copy-start
  7.2 98.3 %all-gather.3.cloned.1.call-start = ((), (), s32[]{:S(2)}) async-start(), calls=%async_computation.5 | async-start | bytes 18063360 | tf_op jit(solution)/shard_map/all_gather | solution.py:123
  10.0 47.8 %copy-start.1 = (f32[2048]{0:T(1024)S(1)}, f32[2048]{0:T(1024)}, u32[]{:S(2)}) copy-start(f32[2048]{0:T(1024)} %param.10) | copy-start | bytes 24580
  10.0 47.8 %copy-start.2 = (f32[2048]{0:T(1024)S(1)}, f32[2048]{0:T(1024)}, u32[]{:S(2)}) copy-start(f32[2048]{0:T(1024)} %param.9) | copy-start | bytes 24580
  57.9 27.5 %copy-start.4 = (s32[256]{0:T(256)S(1)}, s32[256]{0:T(256)}, u32[]{:S(2)}) copy-start(s32[256]{0:T(256)} %param.14) | copy-start | bytes 3076
  81.8 13.3 %all-to-all-start.3 = ((bf16[4,16,4,2048]{3,2,1,0:T(4,128)(2,1)}), bf16[4,16,4,2048]{3,2,1,0:T(4,128)(2,1)S(1)}, u32[]{:S(2)}, u32[]{:S(2)}) async-start(bf16[4,16,4,2048]{3,2,1,0:T(4,128)(2,1)} %broadcast_in_dim.19), calls=%async_computation.3 | async-start | bytes 2097152 | tf_op jit(solution)/shard_map/all_to_all | solution.py:118
  105.5 45.4 %copy-start.3 = (s32[256]{0:T(256)S(1)}, s32[256]{0:T(256)}, u32[]{:S(2)}) copy-start(s32[256]{0:T(256)} %param.13) | copy-start | bytes 3076
  105.5 45.4 %copy-start.5 = (s32[256]{0:T(256)S(1)}, s32[256]{0:T(256)}, u32[]{:S(2)}) copy-start(s32[256]{0:T(256)} %param.15) | copy-start | bytes 3076
  119.0 30.9 %all-to-all-start.4 = ((f32[64,4,4]{2,1,0:T(4,128)}), f32[64,4,4]{2,1,0:T(4,128)S(1)}, u32[]{:S(2)}, u32[]{:S(2)}) async-start(f32[64,4,4]{2,1,0:T(4,128)} %bitcast.5), calls=%async_computation.4 | async-start | bytes 262144 | tf_op jit(solution)/shard_map/all_to_all | solution.py:129
Sparse Core Ops, SparseCore 0:
  10.1 95.2 all-gather.2

commit v8 on v6

--- a/solution.py
+++ b/solution.py
@@ -123,7 +123,11 @@
     blocks = lax.all_gather(head_table, "dp", axis=0, tiled=False)
     vocab_local = head_table.shape[0]
     stats = head_stats(chosen, blocks, targets - position * vocab_local)[:4].T
-    gathered = lax.all_to_all(stats.reshape(devices, owned_count, 4), TENSOR, 0, 0, tiled=True)
+    rings = devices // ring
+    by_y = stats.reshape(rings, ring, owned_count, 4).transpose(1, 0, 2, 3)
+    near = lax.all_to_all(by_y, "ty", 0, 0, tiled=True)
+    gathered = lax.all_to_all(near.transpose(1, 0, 2, 3), "tz", 0, 0, tiled=True)
+    gathered = gathered.reshape(devices, owned_count, 4)
     part_max = gathered[:, :, 0]
     maxima = jnp.max(part_max, axis=0)
     gap = part_max - maxima[None, :]

time: 159 us -> 164 us (1.031)
  blocking collectives: 68.8 us -> 76.7 us
  waiting for transfers between devices: 33.3 us -> 29.8 us
  starting transfers between devices: 18.9 us -> 15.6 us
  local copies, waits for them, and re-layouts: 5.77 us -> 7.47 us
    all_to_all x1 -> x2, blocking collectives: 15.5 us -> 23.5 us  [body(): near = lax.all_to_all(by_y, 'ty', 0, 0, tiled=True)]
    all_to_all x1, waiting for transfers between devices: 14.8 us -> 11.3 us  [body(): lax.all_to_all(near.transpose(1, 0, 2, 3), 'tz', 0, 0, tiled=True)]
    all_to_all x1, starting transfers between devices: 15.4 us -> 12 us  [body(): lax.all_to_all(near.transpose(1, 0, 2, 3), 'tz', 0, 0, tiled=True)]
where the time goes in v8:
time: 164 us; the launch traced here: 161 us
  blocking collectives  76.7 us (47%)
  waiting for transfers between devices  29.8 us (18%)
  starting transfers between devices  15.6 us (10%)
  between operations  14.9 us (9%)
  Pallas kernels  11.5 us (7%)
  local copies, waits for them, and re-layouts  7.47 us (5%)
  other arithmetic  4.88 us (3%)
    all_to_all x1, blocking collectives, body(): arrived = lax.all_to_all(near, 'tz', 0, 0, tiled=True)  31 us
    all_to_all x2, blocking collectives, body(): near = lax.all_to_all(by_y, 'ty', 0, 0, tiled=True)  23.5 us
    all_to_all x1, blocking collectives, body(): lax.all_to_all(jnp.broadcast_to(owned_normed[None], (devices // ring, own...  22.3 us
    all_to_all x1, starting transfers between devices, body(): lax.all_to_all(near.transpose(1, 0, 2, 3), 'tz', 0, 0, tiled=True)  12 us
    pallas_call x1, Pallas kernels, head_stats(): pl.pallas_call(head_stats_kernel, grid=(vocab // tile,), in_specs=[pl.Blo...  11.5 us
    all_to_all x1, waiting for transfers between devices, body(): lax.all_to_all(near.transpose(1, 0, 2, 3), 'tz', 0, 0, tiled=True)  11.3 us
    all_to_all x1, waiting for transfers between devices, body(): lax.all_to_all(jnp.broadcast_to(along_z[None], (ring, devices // ring, ow...  9.15 us
    all_gather x1, waiting for transfers between devices, body(): blocks = lax.all_gather(head_table, 'dp', axis=0, tiled=False)  8.65 us
  transfers between devices with their start and end apart: 3, of which 3 were waited for; matrix products, arithmetic and copies ran while one was open for 5% of the time, Pallas kernels for 0%

profile of v8, /device:TPU:1, one launch (start us, length us, event | category | flops | bytes accessed | tf_op | source)
XLA Modules:
  0.0 161.4 jit_solution(6586543312344529383)
XLA Ops:
  7.2 0.7 all-gather.3.cloned.1.call-update
  7.9 0.7 broadcast_subtract_fusion.1
  8.6 0.5 convolution_convert_fusion
  9.1 0.4 reshape.103
  9.5 0.5 copy.47
  10.0 15.5 %all_to_all.30 = bf16[4,16,4,2048]{3,2,1,0:T(4,128)(2,1)S(1)} all-to-all(bf16[4,16,4,2048]{3,2,1,0:T(4,128)(2,1)S(1)} %bitcast.30), channel_id=1, replica_groups=mesh['dp'=8,'tz'=16,'ty'=4] {'ty'}, dimensions={0} | all-to-all | bytes 2097152 | tf_op jit(solution)/shard_map/all_to_all | solution.py:110
  25.5 0.7 reduce_sum.70
  26.2 31.0 %all_to_all.31 = bf16[16,4,2048]{2,1,0:T(4,128)(2,1)S(1)} all-to-all(bf16[16,4,2048]{2,1,0:T(4,128)(2,1)S(1)} %reduce_sum.70), channel_id=1, replica_groups=mesh['dp'=8,'tz'=16,'ty'=4] {'tz'}, dimensions={0} | all-to-all | bytes 524288 | tf_op jit(solution)/shard_map/all_to_all | solution.py:112
  57.2 0.4 convert_reduce_fusion
  57.6 0.2 multiply_reduce_fusion
  58.0 22.3 %all_to_all.32 = bf16[16,4,2048]{2,1,0:T(4,128)(2,1)S(1)} all-to-all(bf16[16,4,2048]{2,1,0:T(4,128)(2,1)S(1)} %broadcast_in_dim.18), channel_id=1, replica_groups=mesh['dp'=8,'tz'=16,'ty'=4] {'tz'}, dimensions={0} | all-to-all | bytes 524288 | tf_op jit(solution)/shard_map/all_to_all | solution.py:115
  80.3 1.5 broadcast_in_dim.19
  81.8 3.5 %all-to-all-start.3 = ((bf16[4,16,4,2048]{3,2,1,0:T(4,128)(2,1)}), bf16[4,16,4,2048]{3,2,1,0:T(4,128)(2,1)S(1)}, u32[]{:S(2)}, u32[]{:S(2)}) async-start(bf16[4,16,4,2048]{3,2,1,0:T(4,128)(2,1)} %broadcast_in_dim.19), calls=%async_computation.3 | async-start | bytes 2097152 | tf_op jit(solution)/shard_map/all_to_all | solution.py:118
  85.4 0.6 broadcast_subtract_fusion
  86.0 9.1 %all-to-all-done.3 = bf16[4,16,4,2048]{3,2,1,0:T(4,128)(2,1)S(1)} async-done(((bf16[4,16,4,2048]{3,2,1,0:T(4,128)(2,1)}), bf16[4,16,4,2048]{3,2,1,0:T(4,128)(2,1)S(1)}, u32[]{:S(2)}, u32[]{:S(2)}) %all-to-all-start.3) | async-done | bytes 1048608 | tf_op jit(solution)/shard_map/all_to_all | solution.py:118
  95.1 0.6 copy.38
  95.7 1.1 reshape.104.chosen_ref
  96.8 8.6 %all-gather.3.cloned.1.call-done = bf16[31360,256]{1,0:T(8,128)(2,1)} async-done(((bf16[3920,256]{1,0:T(8,128)(2,1)}), bf16[31360,256]{1,0:T(8,128)(2,1)}) %all-gather.3.cloned.1.call-update) | async-done | bytes 16056336 | tf_op jit(solution)/shard_map/all_gather | solution.py:123
  105.5 11.5 %shard_map.95 = f32[8,256]{1,0:T(8,128)} custom-call(bf16[256,2048]{1,0:T(8,128)(2,1)} %reshape.104.chosen_ref, bf16[8,3920,256]{2,1,0:T(8,128)(2,1)} %bitcast.28, s32[1,256]{1,0:T(1,128)} %bitcast.37), custom_call_target="tpu_custom_call" | custom-call | tf_op jit(solution)/shard_map/pallas_call | solution.py:80
  117.0 0.7 slice_bitcast_fusion
  117.7 0.2 reshape.106
  117.9 0.2 copy.39
  118.2 7.9 %all_to_all.33 = f32[4,1,256]{2,1,0:T(1,128)S(1)} all-to-all(f32[4,1,256]{2,1,0:T(1,128)S(1)} %reshape.109), channel_id=1, replica_groups=mesh['dp'=8,'tz'=16,'ty'=4] {'ty'}, dimensions={0} | all-to-all | bytes 8192 | tf_op jit(solution)/shard_map/all_to_all | solution.py:128
  126.2 0.5 broadcast.104
  126.7 0.7 reduce.4
  127.4 0.8 copy.40
  128.2 12.0 %all-to-all-start.5 = ((f32[16,4,4,4]{2,1,3,0:T(4,128)}), f32[16,4,4,4]{2,1,3,0:T(4,128)S(1)}, u32[]{:S(2)}, u32[]{:S(2)}) async-start(f32[16,4,4,4]{2,1,3,0:T(4,128)} %copy.40), calls=%async_computation.5 | async-start | bytes 262144 | tf_op jit(solution)/shard_map/all_to_all | solution.py:129
  140.9 11.3 %all-to-all-done.5 = f32[16,4,4,4]{2,1,3,0:T(4,128)S(1)} async-done(((f32[16,4,4,4]{2,1,3,0:T(4,128)}), f32[16,4,4,4]{2,1,3,0:T(4,128)S(1)}, u32[]{:S(2)}, u32[]{:S(2)}) %all-to-all-start.5) | async-done | bytes 4128 | tf_op jit(solution)/shard_map/all_to_all | solution.py:129
  152.2 0.6 copy.41
  153.2 0.2 multiply_reduce_fusion.1
  153.4 0.6 subtract_select_fusion
  154.0 0.5 subtract_select_fusion.1
  (23 shorter events, 0.8 us)
Async XLA Ops:
  7.2 1.4 copy-start
  7.2 98.3 %all-gather.3.cloned.1.call-start = ((), (), s32[]{:S(2)}) async-start(), calls=%async_computation.6 | async-start | bytes 18063360 | tf_op jit(solution)/shard_map/all_gather | solution.py:123
  10.0 47.8 %copy-start.1 = (f32[2048]{0:T(1024)S(1)}, f32[2048]{0:T(1024)}, u32[]{:S(2)}) copy-start(f32[2048]{0:T(1024)} %param.10) | copy-start | bytes 24580
  10.0 47.8 %copy-start.2 = (f32[2048]{0:T(1024)S(1)}, f32[2048]{0:T(1024)}, u32[]{:S(2)}) copy-start(f32[2048]{0:T(1024)} %param.9) | copy-start | bytes 24580
  57.9 27.5 %copy-start.4 = (s32[256]{0:T(256)S(1)}, s32[256]{0:T(256)}, u32[]{:S(2)}) copy-start(s32[256]{0:T(256)} %param.14) | copy-start | bytes 3076
  81.8 13.3 %all-to-all-start.3 = ((bf16[4,16,4,2048]{3,2,1,0:T(4,128)(2,1)}), bf16[4,16,4,2048]{3,2,1,0:T(4,128)(2,1)S(1)}, u32[]{:S(2)}, u32[]{:S(2)}) async-start(bf16[4,16,4,2048]{3,2,1,0:T(4,128)(2,1)} %broadcast_in_dim.19), calls=%async_computation.3 | async-start | bytes 2097152 | tf_op jit(solution)/shard_map/all_to_all | solution.py:118
  105.5 47.9 %copy-start.3 = (s32[256]{0:T(256)S(1)}, s32[256]{0:T(256)}, u32[]{:S(2)}) copy-start(s32[256]{0:T(256)} %param.13) | copy-start | bytes 3076
  105.5 47.9 %copy-start.5 = (s32[256]{0:T(256)S(1)}, s32[256]{0:T(256)}, u32[]{:S(2)}) copy-start(s32[256]{0:T(256)} %param.15) | copy-start | bytes 3076
  128.2 24.0 %all-to-all-start.5 = ((f32[16,4,4,4]{2,1,3,0:T(4,128)}), f32[16,4,4,4]{2,1,3,0:T(4,128)S(1)}, u32[]{:S(2)}, u32[]{:S(2)}) async-start(f32[16,4,4,4]{2,1,3,0:T(4,128)} %copy.40), calls=%async_computation.5 | async-start | bytes 262144 | tf_op jit(solution)/shard_map/all_to_all | solution.py:129
Sparse Core Ops, SparseCore 0:
  10.1 95.2 all-gather.2

commit v9 on v6

--- a/solution.py
+++ b/solution.py
@@ -123,7 +123,8 @@
     blocks = lax.all_gather(head_table, "dp", axis=0, tiled=False)
     vocab_local = head_table.shape[0]
     stats = head_stats(chosen, blocks, targets - position * vocab_local)[:4].T
-    gathered = lax.all_to_all(stats.reshape(devices, owned_count, 4), TENSOR, 0, 0, tiled=True)
+    gathered = lax.all_to_all(stats.reshape(devices, owned_count * 4), TENSOR, 0, 0, tiled=True)
+    gathered = gathered.reshape(devices, owned_count, 4)
     part_max = gathered[:, :, 0]
     maxima = jnp.max(part_max, axis=0)
     gap = part_max - maxima[None, :]

time: 159 us -> 157 us (0.987)
  waiting for transfers between devices: 33.3 us -> 31.4 us
    all_to_all x1, waiting for transfers between devices: 14.8 us -> 12.9 us  [body(): lax.all_to_all(stats.reshape(devices, owned_count * 4), TENSOR, 0, 0, til...]
where the time goes in v9:
time: 157 us; the launch traced here: 156 us
  blocking collectives  68.8 us (44%)
  waiting for transfers between devices  31.4 us (20%)
  starting transfers between devices  18.9 us (12%)
  between operations  14.8 us (9%)
  Pallas kernels  11.5 us (7%)
  local copies, waits for them, and re-layouts  5.8 us (4%)
  other arithmetic  4.22 us (3%)
    all_to_all x1, blocking collectives, body(): arrived = lax.all_to_all(near, 'tz', 0, 0, tiled=True)  31 us
    all_to_all x1, blocking collectives, body(): lax.all_to_all(jnp.broadcast_to(owned_normed[None], (devices // ring, own...  22.3 us
    all_to_all x1, blocking collectives, body(): near = lax.all_to_all(by_y, 'ty', 0, 0, tiled=True)  15.5 us
    all_to_all x1, starting transfers between devices, body(): lax.all_to_all(stats.reshape(devices, owned_count * 4), TENSOR, 0, 0, til...  15.4 us
    all_to_all x1, waiting for transfers between devices, body(): lax.all_to_all(stats.reshape(devices, owned_count * 4), TENSOR, 0, 0, til...  12.9 us
    pallas_call x1, Pallas kernels, head_stats(): pl.pallas_call(head_stats_kernel, grid=(vocab // tile,), in_specs=[pl.Blo...  11.5 us
    all_to_all x1, waiting for transfers between devices, body(): lax.all_to_all(jnp.broadcast_to(along_z[None], (ring, devices // ring, ow...  9.15 us
    all_gather x1, waiting for transfers between devices, body(): blocks = lax.all_gather(head_table, 'dp', axis=0, tiled=False)  8.65 us
  transfers between devices with their start and end apart: 3, of which 3 were waited for; matrix products, arithmetic and copies ran while one was open for 5% of the time, Pallas kernels for 0%

profile of v9, /device:TPU:1, one launch (start us, length us, event | category | flops | bytes accessed | tf_op | source)
XLA Modules:
  0.0 156.0 jit_solution(12985923547204092556)
XLA Ops:
  7.2 0.7 all-gather.3.cloned.1.call-update
  7.9 0.7 broadcast_subtract_fusion.1
  8.6 0.5 convolution_convert_fusion
  9.1 0.4 reshape.105
  9.5 0.5 copy.46
  10.0 15.5 %all_to_all.29 = bf16[4,16,4,2048]{3,2,1,0:T(4,128)(2,1)S(1)} all-to-all(bf16[4,16,4,2048]{3,2,1,0:T(4,128)(2,1)S(1)} %bitcast.20), channel_id=1, replica_groups=mesh['dp'=8,'tz'=16,'ty'=4] {'ty'}, dimensions={0} | all-to-all | bytes 2097152 | tf_op jit(solution)/shard_map/all_to_all | solution.py:110
  25.5 0.7 reduce_sum.70
  26.2 31.0 %all_to_all.30 = bf16[16,4,2048]{2,1,0:T(4,128)(2,1)S(1)} all-to-all(bf16[16,4,2048]{2,1,0:T(4,128)(2,1)S(1)} %reduce_sum.70), channel_id=1, replica_groups=mesh['dp'=8,'tz'=16,'ty'=4] {'tz'}, dimensions={0} | all-to-all | bytes 524288 | tf_op jit(solution)/shard_map/all_to_all | solution.py:112
  57.2 0.4 convert_reduce_fusion
  57.6 0.2 multiply_reduce_fusion
  57.8 0.1 add_convert_fusion
  57.9 0.1 broadcast_in_dim.18
  58.0 22.3 %all_to_all.31 = bf16[16,4,2048]{2,1,0:T(4,128)(2,1)S(1)} all-to-all(bf16[16,4,2048]{2,1,0:T(4,128)(2,1)S(1)} %broadcast_in_dim.18), channel_id=1, replica_groups=mesh['dp'=8,'tz'=16,'ty'=4] {'tz'}, dimensions={0} | all-to-all | bytes 524288 | tf_op jit(solution)/shard_map/all_to_all | solution.py:115
  80.3 1.5 broadcast_in_dim.19
  81.8 3.5 %all-to-all-start.3 = ((bf16[4,16,4,2048]{3,2,1,0:T(4,128)(2,1)}), bf16[4,16,4,2048]{3,2,1,0:T(4,128)(2,1)S(1)}, u32[]{:S(2)}, u32[]{:S(2)}) async-start(bf16[4,16,4,2048]{3,2,1,0:T(4,128)(2,1)} %broadcast_in_dim.19), calls=%async_computation.3 | async-start | bytes 2097152 | tf_op jit(solution)/shard_map/all_to_all | solution.py:118
  85.4 0.6 broadcast_subtract_fusion
  86.0 9.1 %all-to-all-done.3 = bf16[4,16,4,2048]{3,2,1,0:T(4,128)(2,1)S(1)} async-done(((bf16[4,16,4,2048]{3,2,1,0:T(4,128)(2,1)}), bf16[4,16,4,2048]{3,2,1,0:T(4,128)(2,1)S(1)}, u32[]{:S(2)}, u32[]{:S(2)}) %all-to-all-start.3) | async-done | bytes 1048608 | tf_op jit(solution)/shard_map/all_to_all | solution.py:118
  95.1 0.6 copy.37
  95.7 1.1 reshape.106.chosen_ref
  96.8 8.6 %all-gather.3.cloned.1.call-done = bf16[31360,256]{1,0:T(8,128)(2,1)} async-done(((bf16[3920,256]{1,0:T(8,128)(2,1)}), bf16[31360,256]{1,0:T(8,128)(2,1)}) %all-gather.3.cloned.1.call-update) | async-done | bytes 16056336 | tf_op jit(solution)/shard_map/all_gather | solution.py:123
  105.5 11.5 %shard_map.95 = f32[8,256]{1,0:T(8,128)} custom-call(bf16[256,2048]{1,0:T(8,128)(2,1)} %reshape.106.chosen_ref, bf16[8,3920,256]{2,1,0:T(8,128)(2,1)} %bitcast.18, s32[1,256]{1,0:T(1,128)} %bitcast.26), custom_call_target="tpu_custom_call" | custom-call | tf_op jit(solution)/shard_map/pallas_call | solution.py:80
  117.0 0.7 slice_bitcast_fusion
  117.7 0.1 copy.38
  117.9 0.7 all_to_all.22
  118.6 15.4 %all-to-all-start.4 = ((f32[64,1,16]{2,1,0:T(1,128)}), f32[64,1,16]{2,1,0:T(1,128)S(1)}, u32[]{:S(2)}, u32[]{:S(2)}) async-start(f32[64,1,16]{2,1,0:T(1,128)} %bitcast.6), calls=%async_computation.4 | async-start | bytes 65536 | tf_op jit(solution)/shard_map/all_to_all | solution.py:126
  134.6 12.9 %all-to-all-done.4 = f32[64,1,16]{2,1,0:T(1,128)S(1)} async-done(((f32[64,1,16]{2,1,0:T(1,128)}), f32[64,1,16]{2,1,0:T(1,128)S(1)}, u32[]{:S(2)}, u32[]{:S(2)}) %all-to-all-start.4) | async-done | bytes 4128 | tf_op jit(solution)/shard_map/all_to_all | solution.py:126
  147.6 0.1 copy.40
  147.6 0.1 slice_reduce_fusion
  147.7 0.1 reduce_max.9
  147.9 0.2 multiply_reduce_fusion.1
  148.1 0.6 subtract_select_fusion
  148.7 0.5 subtract_select_fusion.1
  (15 shorter events, 0.1 us)
Async XLA Ops:
  7.2 1.4 copy-start
  7.2 98.3 %all-gather.3.cloned.1.call-start = ((), (), s32[]{:S(2)}) async-start(), calls=%async_computation.5 | async-start | bytes 18063360 | tf_op jit(solution)/shard_map/all_gather | solution.py:123
  10.0 47.8 %copy-start.1 = (f32[2048]{0:T(1024)S(1)}, f32[2048]{0:T(1024)}, u32[]{:S(2)}) copy-start(f32[2048]{0:T(1024)} %param.10) | copy-start | bytes 24580
  10.0 47.8 %copy-start.2 = (f32[2048]{0:T(1024)S(1)}, f32[2048]{0:T(1024)}, u32[]{:S(2)}) copy-start(f32[2048]{0:T(1024)} %param.9) | copy-start | bytes 24580
  57.9 27.5 %copy-start.4 = (s32[256]{0:T(256)S(1)}, s32[256]{0:T(256)}, u32[]{:S(2)}) copy-start(s32[256]{0:T(256)} %param.14) | copy-start | bytes 3076
  81.8 13.3 %all-to-all-start.3 = ((bf16[4,16,4,2048]{3,2,1,0:T(4,128)(2,1)}), bf16[4,16,4,2048]{3,2,1,0:T(4,128)(2,1)S(1)}, u32[]{:S(2)}, u32[]{:S(2)}) async-start(bf16[4,16,4,2048]{3,2,1,0:T(4,128)(2,1)} %broadcast_in_dim.19), calls=%async_computation.3 | async-start | bytes 2097152 | tf_op jit(solution)/shard_map/all_to_all | solution.py:118
  105.5 42.6 %copy-start.3 = (s32[256]{0:T(256)S(1)}, s32[256]{0:T(256)}, u32[]{:S(2)}) copy-start(s32[256]{0:T(256)} %param.13) | copy-start | bytes 3076
  105.5 42.6 %copy-start.5 = (s32[256]{0:T(256)S(1)}, s32[256]{0:T(256)}, u32[]{:S(2)}) copy-start(s32[256]{0:T(256)} %param.15) | copy-start | bytes 3076
  118.6 29.0 %all-to-all-start.4 = ((f32[64,1,16]{2,1,0:T(1,128)}), f32[64,1,16]{2,1,0:T(1,128)S(1)}, u32[]{:S(2)}, u32[]{:S(2)}) async-start(f32[64,1,16]{2,1,0:T(1,128)} %bitcast.6), calls=%async_computation.4 | async-start | bytes 65536 | tf_op jit(solution)/shard_map/all_to_all | solution.py:126
Sparse Core Ops, SparseCore 0:
  10.1 95.2 all-gather.2

commit v10 on v9

--- a/solution.py
+++ b/solution.py
@@ -26,7 +26,7 @@
 
 def tile_of(vocab):
     best = vocab
-    for size in range(8, 641, 8):
+    for size in range(8, 801, 8):
         if vocab % size == 0:
             best = size
     return best

time: 157 us -> 156 us (level)
  no operation moved by 1% of the time
where the time goes in v10:
time: 156 us; the launch traced here: 155 us
  blocking collectives  68.8 us (44%)
  waiting for transfers between devices  31.4 us (20%)
  starting transfers between devices  18.9 us (12%)
  between operations  14.8 us (9%)
  Pallas kernels  10.6 us (7%)
  local copies, waits for them, and re-layouts  5.8 us (4%)
  other arithmetic  4.22 us (3%)
    all_to_all x1, blocking collectives, body(): arrived = lax.all_to_all(near, 'tz', 0, 0, tiled=True)  31 us
    all_to_all x1, blocking collectives, body(): lax.all_to_all(jnp.broadcast_to(owned_normed[None], (devices // ring, own...  22.3 us
    all_to_all x1, blocking collectives, body(): near = lax.all_to_all(by_y, 'ty', 0, 0, tiled=True)  15.5 us
    all_to_all x1, starting transfers between devices, body(): lax.all_to_all(stats.reshape(devices, owned_count * 4), TENSOR, 0, 0, til...  15.4 us
    all_to_all x1, waiting for transfers between devices, body(): lax.all_to_all(stats.reshape(devices, owned_count * 4), TENSOR, 0, 0, til...  12.9 us
    pallas_call x1, Pallas kernels, head_stats(): pl.pallas_call(head_stats_kernel, grid=(vocab // tile,), in_specs=[pl.Blo...  10.6 us
    all_to_all x1, waiting for transfers between devices, body(): lax.all_to_all(jnp.broadcast_to(along_z[None], (ring, devices // ring, ow...  9.15 us
    all_gather x1, waiting for transfers between devices, body(): blocks = lax.all_gather(head_table, 'dp', axis=0, tiled=False)  8.65 us
  transfers between devices with their start and end apart: 3, of which 3 were waited for; matrix products, arithmetic and copies ran while one was open for 5% of the time, Pallas kernels for 0%

profile of v10, /device:TPU:1, one launch (start us, length us, event | category | flops | bytes accessed | tf_op | source)
XLA Modules:
  0.0 155.0 jit_solution(1428964145301473390)
XLA Ops:
  7.2 0.7 all-gather.3.cloned.1.call-update
  7.9 0.7 broadcast_subtract_fusion.1
  8.6 0.5 convolution_convert_fusion
  9.1 0.4 reshape.105
  9.5 0.5 copy.46
  10.0 15.5 %all_to_all.29 = bf16[4,16,4,2048]{3,2,1,0:T(4,128)(2,1)S(1)} all-to-all(bf16[4,16,4,2048]{3,2,1,0:T(4,128)(2,1)S(1)} %bitcast.20), channel_id=1, replica_groups=mesh['dp'=8,'tz'=16,'ty'=4] {'ty'}, dimensions={0} | all-to-all | bytes 2097152 | tf_op jit(solution)/shard_map/all_to_all | solution.py:110
  25.5 0.7 reduce_sum.70
  26.2 31.0 %all_to_all.30 = bf16[16,4,2048]{2,1,0:T(4,128)(2,1)S(1)} all-to-all(bf16[16,4,2048]{2,1,0:T(4,128)(2,1)S(1)} %reduce_sum.70), channel_id=1, replica_groups=mesh['dp'=8,'tz'=16,'ty'=4] {'tz'}, dimensions={0} | all-to-all | bytes 524288 | tf_op jit(solution)/shard_map/all_to_all | solution.py:112
  57.2 0.4 convert_reduce_fusion
  57.6 0.2 multiply_reduce_fusion
  57.8 0.1 add_convert_fusion
  57.9 0.1 broadcast_in_dim.18
  58.0 22.3 %all_to_all.31 = bf16[16,4,2048]{2,1,0:T(4,128)(2,1)S(1)} all-to-all(bf16[16,4,2048]{2,1,0:T(4,128)(2,1)S(1)} %broadcast_in_dim.18), channel_id=1, replica_groups=mesh['dp'=8,'tz'=16,'ty'=4] {'tz'}, dimensions={0} | all-to-all | bytes 524288 | tf_op jit(solution)/shard_map/all_to_all | solution.py:115
  80.3 1.5 broadcast_in_dim.19
  81.8 3.5 %all-to-all-start.3 = ((bf16[4,16,4,2048]{3,2,1,0:T(4,128)(2,1)}), bf16[4,16,4,2048]{3,2,1,0:T(4,128)(2,1)S(1)}, u32[]{:S(2)}, u32[]{:S(2)}) async-start(bf16[4,16,4,2048]{3,2,1,0:T(4,128)(2,1)} %broadcast_in_dim.19), calls=%async_computation.3 | async-start | bytes 2097152 | tf_op jit(solution)/shard_map/all_to_all | solution.py:118
  85.4 0.6 broadcast_subtract_fusion
  86.0 9.1 %all-to-all-done.3 = bf16[4,16,4,2048]{3,2,1,0:T(4,128)(2,1)S(1)} async-done(((bf16[4,16,4,2048]{3,2,1,0:T(4,128)(2,1)}), bf16[4,16,4,2048]{3,2,1,0:T(4,128)(2,1)S(1)}, u32[]{:S(2)}, u32[]{:S(2)}) %all-to-all-start.3) | async-done | bytes 1048608 | tf_op jit(solution)/shard_map/all_to_all | solution.py:118
  95.1 0.6 copy.37
  95.7 1.1 reshape.106.chosen_ref
  96.8 8.6 %all-gather.3.cloned.1.call-done = bf16[31360,256]{1,0:T(8,128)(2,1)} async-done(((bf16[3920,256]{1,0:T(8,128)(2,1)}), bf16[31360,256]{1,0:T(8,128)(2,1)}) %all-gather.3.cloned.1.call-update) | async-done | bytes 16056336 | tf_op jit(solution)/shard_map/all_gather | solution.py:123
  105.5 10.6 %shard_map.95 = f32[8,256]{1,0:T(8,128)} custom-call(bf16[256,2048]{1,0:T(8,128)(2,1)} %reshape.106.chosen_ref, bf16[8,3920,256]{2,1,0:T(8,128)(2,1)} %bitcast.18, s32[1,256]{1,0:T(1,128)} %bitcast.26), custom_call_target="tpu_custom_call" | custom-call | tf_op jit(solution)/shard_map/pallas_call | solution.py:80
  116.0 0.7 slice_bitcast_fusion
  116.7 0.1 copy.38
  116.9 0.7 all_to_all.22
  117.6 15.4 %all-to-all-start.4 = ((f32[64,1,16]{2,1,0:T(1,128)}), f32[64,1,16]{2,1,0:T(1,128)S(1)}, u32[]{:S(2)}, u32[]{:S(2)}) async-start(f32[64,1,16]{2,1,0:T(1,128)} %bitcast.6), calls=%async_computation.4 | async-start | bytes 65536 | tf_op jit(solution)/shard_map/all_to_all | solution.py:126
  133.6 12.9 %all-to-all-done.4 = f32[64,1,16]{2,1,0:T(1,128)S(1)} async-done(((f32[64,1,16]{2,1,0:T(1,128)}), f32[64,1,16]{2,1,0:T(1,128)S(1)}, u32[]{:S(2)}, u32[]{:S(2)}) %all-to-all-start.4) | async-done | bytes 4128 | tf_op jit(solution)/shard_map/all_to_all | solution.py:126
  146.5 0.1 copy.40
  146.6 0.1 slice_reduce_fusion
  146.7 0.1 reduce_max.9
  146.8 0.2 multiply_reduce_fusion.1
  147.1 0.6 subtract_select_fusion
  147.7 0.5 subtract_select_fusion.1
  (15 shorter events, 0.1 us)
Async XLA Ops:
  7.2 1.4 copy-start
  7.2 98.3 %all-gather.3.cloned.1.call-start = ((), (), s32[]{:S(2)}) async-start(), calls=%async_computation.5 | async-start | bytes 18063360 | tf_op jit(solution)/shard_map/all_gather | solution.py:123
  10.0 47.8 %copy-start.1 = (f32[2048]{0:T(1024)S(1)}, f32[2048]{0:T(1024)}, u32[]{:S(2)}) copy-start(f32[2048]{0:T(1024)} %param.10) | copy-start | bytes 24580
  10.0 47.8 %copy-start.2 = (f32[2048]{0:T(1024)S(1)}, f32[2048]{0:T(1024)}, u32[]{:S(2)}) copy-start(f32[2048]{0:T(1024)} %param.9) | copy-start | bytes 24580
  57.9 27.5 %copy-start.4 = (s32[256]{0:T(256)S(1)}, s32[256]{0:T(256)}, u32[]{:S(2)}) copy-start(s32[256]{0:T(256)} %param.14) | copy-start | bytes 3076
  81.8 13.3 %all-to-all-start.3 = ((bf16[4,16,4,2048]{3,2,1,0:T(4,128)(2,1)}), bf16[4,16,4,2048]{3,2,1,0:T(4,128)(2,1)S(1)}, u32[]{:S(2)}, u32[]{:S(2)}) async-start(bf16[4,16,4,2048]{3,2,1,0:T(4,128)(2,1)} %broadcast_in_dim.19), calls=%async_computation.3 | async-start | bytes 2097152 | tf_op jit(solution)/shard_map/all_to_all | solution.py:118
  105.5 41.6 %copy-start.3 = (s32[256]{0:T(256)S(1)}, s32[256]{0:T(256)}, u32[]{:S(2)}) copy-start(s32[256]{0:T(256)} %param.13) | copy-start | bytes 3076
  105.5 41.6 %copy-start.5 = (s32[256]{0:T(256)S(1)}, s32[256]{0:T(256)}, u32[]{:S(2)}) copy-start(s32[256]{0:T(256)} %param.15) | copy-start | bytes 3076
  117.6 29.0 %all-to-all-start.4 = ((f32[64,1,16]{2,1,0:T(1,128)}), f32[64,1,16]{2,1,0:T(1,128)S(1)}, u32[]{:S(2)}, u32[]{:S(2)}) async-start(f32[64,1,16]{2,1,0:T(1,128)} %bitcast.6), calls=%async_computation.4 | async-start | bytes 65536 | tf_op jit(solution)/shard_map/all_to_all | solution.py:126
Sparse Core Ops, SparseCore 0:
  10.1 95.2 all-gather.2

commit v11 on v10

--- a/solution.py
+++ b/solution.py
@@ -26,7 +26,7 @@
 
 def tile_of(vocab):
     best = vocab
-    for size in range(8, 801, 8):
+    for size in range(8, 2001, 8):
         if vocab % size == 0:
             best = size
     return best

time: 156 us -> 155 us (level)
  no operation moved by 1% of the time
where the time goes in v11:
time: 155 us; the launch traced here: 154 us
  blocking collectives  68.8 us (44%)
  waiting for transfers between devices  31.4 us (20%)
  starting transfers between devices  18.9 us (12%)
  between operations  14.8 us (10%)
  Pallas kernels  9.99 us (6%)
  local copies, waits for them, and re-layouts  5.8 us (4%)
  other arithmetic  4.22 us (3%)
    all_to_all x1, blocking collectives, body(): arrived = lax.all_to_all(near, 'tz', 0, 0, tiled=True)  31 us
    all_to_all x1, blocking collectives, body(): lax.all_to_all(jnp.broadcast_to(owned_normed[None], (devices // ring, own...  22.3 us
    all_to_all x1, blocking collectives, body(): near = lax.all_to_all(by_y, 'ty', 0, 0, tiled=True)  15.5 us
    all_to_all x1, starting transfers between devices, body(): lax.all_to_all(stats.reshape(devices, owned_count * 4), TENSOR, 0, 0, til...  15.4 us
    all_to_all x1, waiting for transfers between devices, body(): lax.all_to_all(stats.reshape(devices, owned_count * 4), TENSOR, 0, 0, til...  12.9 us
    pallas_call x1, Pallas kernels, head_stats(): pl.pallas_call(head_stats_kernel, grid=(vocab // tile,), in_specs=[pl.Blo...  9.99 us
    all_to_all x1, waiting for transfers between devices, body(): lax.all_to_all(jnp.broadcast_to(along_z[None], (ring, devices // ring, ow...  9.15 us
    all_gather x1, waiting for transfers between devices, body(): blocks = lax.all_gather(head_table, 'dp', axis=0, tiled=False)  8.65 us
  transfers between devices with their start and end apart: 3, of which 3 were waited for; matrix products, arithmetic and copies ran while one was open for 5% of the time, Pallas kernels for 0%

profile of v11, /device:TPU:1, one launch (start us, length us, event | category | flops | bytes accessed | tf_op | source)
XLA Modules:
  0.0 154.5 jit_solution(5918184359558921590)
XLA Ops:
  7.2 0.7 all-gather.3.cloned.1.call-update
  7.9 0.7 broadcast_subtract_fusion.1
  8.6 0.5 convolution_convert_fusion
  9.1 0.4 reshape.105
  9.5 0.5 copy.46
  10.0 15.5 %all_to_all.29 = bf16[4,16,4,2048]{3,2,1,0:T(4,128)(2,1)S(1)} all-to-all(bf16[4,16,4,2048]{3,2,1,0:T(4,128)(2,1)S(1)} %bitcast.20), channel_id=1, replica_groups=mesh['dp'=8,'tz'=16,'ty'=4] {'ty'}, dimensions={0} | all-to-all | bytes 2097152 | tf_op jit(solution)/shard_map/all_to_all | solution.py:110
  25.5 0.7 reduce_sum.70
  26.2 31.0 %all_to_all.30 = bf16[16,4,2048]{2,1,0:T(4,128)(2,1)S(1)} all-to-all(bf16[16,4,2048]{2,1,0:T(4,128)(2,1)S(1)} %reduce_sum.70), channel_id=1, replica_groups=mesh['dp'=8,'tz'=16,'ty'=4] {'tz'}, dimensions={0} | all-to-all | bytes 524288 | tf_op jit(solution)/shard_map/all_to_all | solution.py:112
  57.2 0.4 convert_reduce_fusion
  57.6 0.2 multiply_reduce_fusion
  57.8 0.1 add_convert_fusion
  57.9 0.1 broadcast_in_dim.18
  58.0 22.3 %all_to_all.31 = bf16[16,4,2048]{2,1,0:T(4,128)(2,1)S(1)} all-to-all(bf16[16,4,2048]{2,1,0:T(4,128)(2,1)S(1)} %broadcast_in_dim.18), channel_id=1, replica_groups=mesh['dp'=8,'tz'=16,'ty'=4] {'tz'}, dimensions={0} | all-to-all | bytes 524288 | tf_op jit(solution)/shard_map/all_to_all | solution.py:115
  80.3 1.5 broadcast_in_dim.19
  81.8 3.5 %all-to-all-start.3 = ((bf16[4,16,4,2048]{3,2,1,0:T(4,128)(2,1)}), bf16[4,16,4,2048]{3,2,1,0:T(4,128)(2,1)S(1)}, u32[]{:S(2)}, u32[]{:S(2)}) async-start(bf16[4,16,4,2048]{3,2,1,0:T(4,128)(2,1)} %broadcast_in_dim.19), calls=%async_computation.3 | async-start | bytes 2097152 | tf_op jit(solution)/shard_map/all_to_all | solution.py:118
  85.4 0.6 broadcast_subtract_fusion
  86.0 9.1 %all-to-all-done.3 = bf16[4,16,4,2048]{3,2,1,0:T(4,128)(2,1)S(1)} async-done(((bf16[4,16,4,2048]{3,2,1,0:T(4,128)(2,1)}), bf16[4,16,4,2048]{3,2,1,0:T(4,128)(2,1)S(1)}, u32[]{:S(2)}, u32[]{:S(2)}) %all-to-all-start.3) | async-done | bytes 1048608 | tf_op jit(solution)/shard_map/all_to_all | solution.py:118
  95.1 0.6 copy.37
  95.7 1.1 reshape.106.chosen_ref
  96.8 8.6 %all-gather.3.cloned.1.call-done = bf16[31360,256]{1,0:T(8,128)(2,1)} async-done(((bf16[3920,256]{1,0:T(8,128)(2,1)}), bf16[31360,256]{1,0:T(8,128)(2,1)}) %all-gather.3.cloned.1.call-update) | async-done | bytes 16056336 | tf_op jit(solution)/shard_map/all_gather | solution.py:123
  105.5 10.0 %shard_map.95 = f32[8,256]{1,0:T(8,128)} custom-call(bf16[256,2048]{1,0:T(8,128)(2,1)} %reshape.106.chosen_ref, bf16[8,3920,256]{2,1,0:T(8,128)(2,1)} %bitcast.18, s32[1,256]{1,0:T(1,128)} %bitcast.26), custom_call_target="tpu_custom_call" | custom-call | tf_op jit(solution)/shard_map/pallas_call | solution.py:80
  115.5 0.7 slice_bitcast_fusion
  116.2 0.1 copy.38
  116.3 0.7 all_to_all.22
  117.0 15.4 %all-to-all-start.4 = ((f32[64,1,16]{2,1,0:T(1,128)}), f32[64,1,16]{2,1,0:T(1,128)S(1)}, u32[]{:S(2)}, u32[]{:S(2)}) async-start(f32[64,1,16]{2,1,0:T(1,128)} %bitcast.6), calls=%async_computation.4 | async-start | bytes 65536 | tf_op jit(solution)/shard_map/all_to_all | solution.py:126
  133.0 12.9 %all-to-all-done.4 = f32[64,1,16]{2,1,0:T(1,128)S(1)} async-done(((f32[64,1,16]{2,1,0:T(1,128)}), f32[64,1,16]{2,1,0:T(1,128)S(1)}, u32[]{:S(2)}, u32[]{:S(2)}) %all-to-all-start.4) | async-done | bytes 4128 | tf_op jit(solution)/shard_map/all_to_all | solution.py:126
  146.0 0.1 copy.40
  146.0 0.1 slice_reduce_fusion
  146.2 0.1 reduce_max.9
  146.3 0.2 multiply_reduce_fusion.1
  146.5 0.6 subtract_select_fusion
  147.1 0.5 subtract_select_fusion.1
  (15 shorter events, 0.1 us)
Async XLA Ops:
  7.2 1.4 copy-start
  7.2 98.3 %all-gather.3.cloned.1.call-start = ((), (), s32[]{:S(2)}) async-start(), calls=%async_computation.5 | async-start | bytes 18063360 | tf_op jit(solution)/shard_map/all_gather | solution.py:123
  10.0 47.8 %copy-start.1 = (f32[2048]{0:T(1024)S(1)}, f32[2048]{0:T(1024)}, u32[]{:S(2)}) copy-start(f32[2048]{0:T(1024)} %param.10) | copy-start | bytes 24580
  10.0 47.8 %copy-start.2 = (f32[2048]{0:T(1024)S(1)}, f32[2048]{0:T(1024)}, u32[]{:S(2)}) copy-start(f32[2048]{0:T(1024)} %param.9) | copy-start | bytes 24580
  57.9 27.5 %copy-start.4 = (s32[256]{0:T(256)S(1)}, s32[256]{0:T(256)}, u32[]{:S(2)}) copy-start(s32[256]{0:T(256)} %param.14) | copy-start | bytes 3076
  81.8 13.3 %all-to-all-start.3 = ((bf16[4,16,4,2048]{3,2,1,0:T(4,128)(2,1)}), bf16[4,16,4,2048]{3,2,1,0:T(4,128)(2,1)S(1)}, u32[]{:S(2)}, u32[]{:S(2)}) async-start(bf16[4,16,4,2048]{3,2,1,0:T(4,128)(2,1)} %broadcast_in_dim.19), calls=%async_computation.3 | async-start | bytes 2097152 | tf_op jit(solution)/shard_map/all_to_all | solution.py:118
  105.5 41.0 %copy-start.3 = (s32[256]{0:T(256)S(1)}, s32[256]{0:T(256)}, u32[]{:S(2)}) copy-start(s32[256]{0:T(256)} %param.13) | copy-start | bytes 3076
  105.5 41.0 %copy-start.5 = (s32[256]{0:T(256)S(1)}, s32[256]{0:T(256)}, u32[]{:S(2)}) copy-start(s32[256]{0:T(256)} %param.15) | copy-start | bytes 3076
  117.0 29.0 %all-to-all-start.4 = ((f32[64,1,16]{2,1,0:T(1,128)}), f32[64,1,16]{2,1,0:T(1,128)S(1)}, u32[]{:S(2)}, u32[]{:S(2)}) async-start(f32[64,1,16]{2,1,0:T(1,128)} %bitcast.6), calls=%async_computation.4 | async-start | bytes 65536 | tf_op jit(solution)/shard_map/all_to_all | solution.py:126
Sparse Core Ops, SparseCore 0:
  10.1 95.2 all-gather.2

commit v12 on v11

--- a/solution.py
+++ b/solution.py
@@ -26,7 +26,7 @@
 
 def tile_of(vocab):
     best = vocab
-    for size in range(8, 2001, 8):
+    for size in range(8, 4001, 8):
         if vocab % size == 0:
             best = size
     return best

time: 155 us -> 157 us (1.013)
  Pallas kernels: 9.99 us -> 12.5 us
    pallas_call x1, Pallas kernels: 9.99 us -> 12.5 us  [head_stats(): pl.pallas_call(head_stats_kernel, grid=(vocab // tile,), in_specs=[pl.Blo...]
where the time goes in v12:
time: 157 us
  blocking collectives  68.8 us (44%)
  waiting for transfers between devices  31.4 us (20%)
  starting transfers between devices  18.9 us (12%)
  between operations  14.8 us (9%)
  Pallas kernels  12.5 us (8%)
  local copies, waits for them, and re-layouts  5.8 us (4%)
  other arithmetic  4.22 us (3%)
    all_to_all x1, blocking collectives, body(): arrived = lax.all_to_all(near, 'tz', 0, 0, tiled=True)  31 us
    all_to_all x1, blocking collectives, body(): lax.all_to_all(jnp.broadcast_to(owned_normed[None], (devices // ring, own...  22.3 us
    all_to_all x1, blocking collectives, body(): near = lax.all_to_all(by_y, 'ty', 0, 0, tiled=True)  15.5 us
    all_to_all x1, starting transfers between devices, body(): lax.all_to_all(stats.reshape(devices, owned_count * 4), TENSOR, 0, 0, til...  15.4 us
    all_to_all x1, waiting for transfers between devices, body(): lax.all_to_all(stats.reshape(devices, owned_count * 4), TENSOR, 0, 0, til...  12.9 us
    pallas_call x1, Pallas kernels, head_stats(): pl.pallas_call(head_stats_kernel, grid=(vocab // tile,), in_specs=[pl.Blo...  12.5 us
    all_to_all x1, waiting for transfers between devices, body(): lax.all_to_all(jnp.broadcast_to(along_z[None], (ring, devices // ring, ow...  9.15 us
    all_gather x1, waiting for transfers between devices, body(): blocks = lax.all_gather(head_table, 'dp', axis=0, tiled=False)  8.65 us
  transfers between devices with their start and end apart: 3, of which 3 were waited for; matrix products, arithmetic and copies ran while one was open for 5% of the time, Pallas kernels for 0%

profile of v12, /device:TPU:1, one launch (start us, length us, event | category | flops | bytes accessed | tf_op | source)
XLA Modules:
  0.0 157.0 jit_solution(12477537266464176527)
XLA Ops:
  7.2 0.7 all-gather.3.cloned.1.call-update
  7.9 0.7 broadcast_subtract_fusion.1
  8.6 0.5 convolution_convert_fusion
  9.1 0.4 reshape.105
  9.5 0.5 copy.46
  10.0 15.5 %all_to_all.29 = bf16[4,16,4,2048]{3,2,1,0:T(4,128)(2,1)S(1)} all-to-all(bf16[4,16,4,2048]{3,2,1,0:T(4,128)(2,1)S(1)} %bitcast.20), channel_id=1, replica_groups=mesh['dp'=8,'tz'=16,'ty'=4] {'ty'}, dimensions={0} | all-to-all | bytes 2097152 | tf_op jit(solution)/shard_map/all_to_all | solution.py:110
  25.5 0.7 reduce_sum.70
  26.2 31.0 %all_to_all.30 = bf16[16,4,2048]{2,1,0:T(4,128)(2,1)S(1)} all-to-all(bf16[16,4,2048]{2,1,0:T(4,128)(2,1)S(1)} %reduce_sum.70), channel_id=1, replica_groups=mesh['dp'=8,'tz'=16,'ty'=4] {'tz'}, dimensions={0} | all-to-all | bytes 524288 | tf_op jit(solution)/shard_map/all_to_all | solution.py:112
  57.2 0.4 convert_reduce_fusion
  57.6 0.2 multiply_reduce_fusion
  57.8 0.1 add_convert_fusion
  57.9 0.1 broadcast_in_dim.18
  58.0 22.3 %all_to_all.31 = bf16[16,4,2048]{2,1,0:T(4,128)(2,1)S(1)} all-to-all(bf16[16,4,2048]{2,1,0:T(4,128)(2,1)S(1)} %broadcast_in_dim.18), channel_id=1, replica_groups=mesh['dp'=8,'tz'=16,'ty'=4] {'tz'}, dimensions={0} | all-to-all | bytes 524288 | tf_op jit(solution)/shard_map/all_to_all | solution.py:115
  80.3 1.5 broadcast_in_dim.19
  81.8 3.5 %all-to-all-start.3 = ((bf16[4,16,4,2048]{3,2,1,0:T(4,128)(2,1)}), bf16[4,16,4,2048]{3,2,1,0:T(4,128)(2,1)S(1)}, u32[]{:S(2)}, u32[]{:S(2)}) async-start(bf16[4,16,4,2048]{3,2,1,0:T(4,128)(2,1)} %broadcast_in_dim.19), calls=%async_computation.3 | async-start | bytes 2097152 | tf_op jit(solution)/shard_map/all_to_all | solution.py:118
  85.4 0.6 broadcast_subtract_fusion
  86.0 9.1 %all-to-all-done.3 = bf16[4,16,4,2048]{3,2,1,0:T(4,128)(2,1)S(1)} async-done(((bf16[4,16,4,2048]{3,2,1,0:T(4,128)(2,1)}), bf16[4,16,4,2048]{3,2,1,0:T(4,128)(2,1)S(1)}, u32[]{:S(2)}, u32[]{:S(2)}) %all-to-all-start.3) | async-done | bytes 1048608 | tf_op jit(solution)/shard_map/all_to_all | solution.py:118
  95.1 0.6 copy.37
  95.7 1.1 reshape.106.chosen_ref
  96.8 8.6 %all-gather.3.cloned.1.call-done = bf16[31360,256]{1,0:T(8,128)(2,1)} async-done(((bf16[3920,256]{1,0:T(8,128)(2,1)}), bf16[31360,256]{1,0:T(8,128)(2,1)}) %all-gather.3.cloned.1.call-update) | async-done | bytes 16056336 | tf_op jit(solution)/shard_map/all_gather | solution.py:123
  105.5 12.5 %shard_map.95 = f32[8,256]{1,0:T(8,128)} custom-call(bf16[256,2048]{1,0:T(8,128)(2,1)} %reshape.106.chosen_ref, bf16[8,3920,256]{2,1,0:T(8,128)(2,1)} %bitcast.18, s32[1,256]{1,0:T(1,128)} %bitcast.26), custom_call_target="tpu_custom_call" | custom-call | tf_op jit(solution)/shard_map/pallas_call | solution.py:80
  118.0 0.7 slice_bitcast_fusion
  118.7 0.1 copy.38
  118.9 0.7 all_to_all.22
  119.6 15.4 %all-to-all-start.4 = ((f32[64,1,16]{2,1,0:T(1,128)}), f32[64,1,16]{2,1,0:T(1,128)S(1)}, u32[]{:S(2)}, u32[]{:S(2)}) async-start(f32[64,1,16]{2,1,0:T(1,128)} %bitcast.6), calls=%async_computation.4 | async-start | bytes 65536 | tf_op jit(solution)/shard_map/all_to_all | solution.py:126
  135.6 12.9 %all-to-all-done.4 = f32[64,1,16]{2,1,0:T(1,128)S(1)} async-done(((f32[64,1,16]{2,1,0:T(1,128)}), f32[64,1,16]{2,1,0:T(1,128)S(1)}, u32[]{:S(2)}, u32[]{:S(2)}) %all-to-all-start.4) | async-done | bytes 4128 | tf_op jit(solution)/shard_map/all_to_all | solution.py:126
  148.5 0.1 copy.40
  148.6 0.1 slice_reduce_fusion
  148.7 0.1 reduce_max.9
  148.8 0.2 multiply_reduce_fusion.1
  149.1 0.6 subtract_select_fusion
  149.7 0.5 subtract_select_fusion.1
  (15 shorter events, 0.1 us)
Async XLA Ops:
  7.2 1.4 copy-start
  7.2 98.3 %all-gather.3.cloned.1.call-start = ((), (), s32[]{:S(2)}) async-start(), calls=%async_computation.5 | async-start | bytes 18063360 | tf_op jit(solution)/shard_map/all_gather | solution.py:123
  10.0 47.8 %copy-start.1 = (f32[2048]{0:T(1024)S(1)}, f32[2048]{0:T(1024)}, u32[]{:S(2)}) copy-start(f32[2048]{0:T(1024)} %param.10) | copy-start | bytes 24580
  10.0 47.8 %copy-start.2 = (f32[2048]{0:T(1024)S(1)}, f32[2048]{0:T(1024)}, u32[]{:S(2)}) copy-start(f32[2048]{0:T(1024)} %param.9) | copy-start | bytes 24580
  57.9 27.5 %copy-start.4 = (s32[256]{0:T(256)S(1)}, s32[256]{0:T(256)}, u32[]{:S(2)}) copy-start(s32[256]{0:T(256)} %param.14) | copy-start | bytes 3076
  81.8 13.3 %all-to-all-start.3 = ((bf16[4,16,4,2048]{3,2,1,0:T(4,128)(2,1)}), bf16[4,16,4,2048]{3,2,1,0:T(4,128)(2,1)S(1)}, u32[]{:S(2)}, u32[]{:S(2)}) async-start(bf16[4,16,4,2048]{3,2,1,0:T(4,128)(2,1)} %broadcast_in_dim.19), calls=%async_computation.3 | async-start | bytes 2097152 | tf_op jit(solution)/shard_map/all_to_all | solution.py:118
  105.5 43.6 %copy-start.3 = (s32[256]{0:T(256)S(1)}, s32[256]{0:T(256)}, u32[]{:S(2)}) copy-start(s32[256]{0:T(256)} %param.13) | copy-start | bytes 3076
  105.5 43.6 %copy-start.5 = (s32[256]{0:T(256)S(1)}, s32[256]{0:T(256)}, u32[]{:S(2)}) copy-start(s32[256]{0:T(256)} %param.15) | copy-start | bytes 3076
  119.6 29.0 %all-to-all-start.4 = ((f32[64,1,16]{2,1,0:T(1,128)}), f32[64,1,16]{2,1,0:T(1,128)S(1)}, u32[]{:S(2)}, u32[]{:S(2)}) async-start(f32[64,1,16]{2,1,0:T(1,128)} %bitcast.6), calls=%async_computation.4 | async-start | bytes 65536 | tf_op jit(solution)/shard_map/all_to_all | solution.py:126
Sparse Core Ops, SparseCore 0:
  10.1 95.2 all-gather.2
